TPU v7x, 32 devices: a whole 2x2x4 slice. The times are simulated.
32 devices in a mesh: job: 2 (over x), space: 4 (over y, core), arc: 4 (over z).
Axes of the slice: x: 2, y: 2, z: 4, core: 2. Of those that a mesh axis runs over, the one named last changes fastest.
Arguments:
- saved_velocity_trajectory: bfloat16 [64, 3, 8, 128, 128], P(('job', 'arc'), None, 'space'), parts along dimension 0, may hold values from -4 to 4
- saved_warmth_trajectory: bfloat16 [64, 8, 128, 128], P(('job', 'arc'), 'space'), parts along dimension 0, may hold values from -5 to 5
- control_porosity: float32 [16, 128, 128], P(('job', 'space')), parts along dimension 0, may hold values from 0.05 to 1
- control_volume_flag: int32 [16, 128, 128], P(('job', 'space')), parts along dimension 0, may hold values 0 or 1
- entrance_face_flag: int32 [256, 128], P('job'), parts along dimension 0, may hold values 0 or 1
Outputs:
- gradient: float32 [16, 128, 128], P(('job', 'space'), 'arc'), parts along dimension 0
- entry_adjoint: float32 [8, 4, 8, 128, 128], P(('job', 'arc'), None, 'space'), parts along dimension 0
There are 2 independent parts, one for each index of `job`. A program takes and returns all parts, laid end to end along the dimension named above; each array names one. Nothing has to cross between parts.
All inputs are finite; a program needn't handle non-finite values. No bound on the sum of `control_volume_flag` on one device may be relied on, other than what follows from the above.
Results may differ from a plain program's by a relative error of at most 0.0003.
Values may be sent and summed in bfloat16 or wider, within the bound.
No kernel may reach another device: no remote copies, remote signals or barrier semaphores. Data moves between devices by JAX's collectives and lax.ppermute only.
A program may use at most 64 MiB of HBM per device.

v0:
```python
import jax
import jax.numpy as jnp
from jax import lax
from jax.experimental import pallas as pl
from jax.experimental.pallas import tpu as pltpu
from jax.sharding import PartitionSpec as P


def padded(cells, sides, width):
    for axis, dim in sides:
        count = lax.axis_size(axis)
        ends = count - 1
        head = lax.slice_in_dim(cells, 0, width, axis=dim)
        tail = lax.slice_in_dim(cells, cells.shape[dim] - width, cells.shape[dim], axis=dim)
        cells = jnp.concatenate(
            [
                lax.ppermute(tail, axis, [(i, (i + 1) % count) for i in range(ends)]),
                cells,
                lax.ppermute(head, axis, [((i + 1) % count, i) for i in range(ends)]),
            ],
            axis=dim,
        )
    return cells


def passed_along(value, axis, steps):
    count = lax.axis_size(axis)
    pairs = [(source, (source + steps) % count) for source in range(count)]
    return lax.ppermute(value, axis, pairs)


def laplace(ext):
    mid = ext[..., 1:-1, 1:-1, 1:-1]
    total = ext[..., 2:, 1:-1, 1:-1] + ext[..., :-2, 1:-1, 1:-1]
    total = total + ext[..., 1:-1, 2:, 1:-1] + ext[..., 1:-1, :-2, 1:-1]
    total = total + ext[..., 1:-1, 1:-1, 2:] + ext[..., 1:-1, 1:-1, :-2]
    return total - 6.0 * mid


def slopes(ext):
    return (
        0.5 * (ext[..., 2:, 1:-1, 1:-1] - ext[..., :-2, 1:-1, 1:-1]),
        0.5 * (ext[..., 1:-1, 2:, 1:-1] - ext[..., 1:-1, :-2, 1:-1]),
        0.5 * (ext[..., 1:-1, 1:-1, 2:] - ext[..., 1:-1, 1:-1, :-2]),
    )


def pad_sides(field, operating_variant):
    widths = [(0, 0)] * (field.ndim - 2) + [(1, 1), (1, 1)]
    return jnp.pad(field, widths, mode=operating_variant)


def adjoint_update(
    adj,
    ext_a,
    ext_b,
    padded_thermal_field,
    speed,
    alpha,
    porosity_sensitivity,
    solid,
    quadrature_factor,
):
    a_now = adj[:3]
    current_adjoint_vector = adj[3]
    grad_b = slopes(ext_b)
    grad_a = slopes(ext_a)
    grad_t = slopes(padded_thermal_field)
    carry_b = speed[0] * grad_b[0] + speed[1] * grad_b[1] + speed[2] * grad_b[2]
    carry_a = speed[0:1] * grad_a[0] + speed[1:2] * grad_a[1] + speed[2:3] * grad_a[2]
    thermal_current_field = padded_thermal_field[1:-1, 1:-1, 1:-1]
    grad_stack = jnp.stack(grad_t)
    new_a = a_now + 0.1 * (
        1.2 * laplace(ext_a) + carry_a - alpha * a_now - current_adjoint_vector * grad_stack
    )
    new_b = current_adjoint_vector + 0.1 * (
        1.2 * laplace(ext_b) + carry_b - 2.0 * solid * current_adjoint_vector + 2.0 * solid
    )
    common_divisor_lcm_like = jnp.sum(a_now * speed, axis=0)
    summand_contribution = (
        0.1
        * quadrature_factor
        * (
            porosity_sensitivity * common_divisor_lcm_like
            + 2.0 * (current_adjoint_vector - 1.0) * thermal_current_field
        )
    )
    return (jnp.concatenate([new_a, new_b[None]], axis=0), summand_contribution)


def halo_body(
    saved_velocity_trajectory,
    saved_warmth_trajectory,
    control_porosity,
    control_volume_flag,
    entrance_face_flag,
):
    quadrature_factor = control_volume_flag.astype(jnp.float32)
    gamma = jnp.where(control_volume_flag == 1, control_porosity, jnp.float32(0.0))
    solid = 1.0 - gamma
    alpha = 3.0 * 0.1 * solid / (0.1 + gamma)
    porosity_sensitivity = -3.0 * 0.1 * 1.1 / ((0.1 + gamma) * (0.1 + gamma))
    leading_plane = lax.axis_index("space") == 0
    trailing_plane = lax.axis_index("space") == lax.axis_size("space") - 1
    device_instant_total = saved_warmth_trajectory.shape[0]
    cycle_ext = padded(saved_warmth_trajectory, (("space", 1),), 1)

    def closing_thermal_value(thermal_current_field, with_halo_padding):
        floor_limit = jnp.where(leading_plane, thermal_current_field[0], with_halo_padding[0])
        ceiling_bound = jnp.where(trailing_plane, thermal_current_field[-1], with_halo_padding[-1])
        return pad_sides(
            jnp.concatenate(
                [floor_limit[None], thermal_current_field, ceiling_bound[None]], axis=0
            ),
            "edge",
        )

    def one_step(adj, interior_block):
        speed = saved_velocity_trajectory[interior_block].astype(jnp.float32)
        thermal_current_field = saved_warmth_trajectory[interior_block].astype(jnp.float32)
        with_halo_padding = padded(adj, (("space", 1),), 1)
        thermal_halo_values = cycle_ext[interior_block].astype(jnp.float32)
        complete_thermal_field = jnp.concatenate(
            [thermal_halo_values[:1], thermal_current_field, thermal_halo_values[-1:]], axis=0
        )
        padded_thermal_field = closing_thermal_value(thermal_current_field, complete_thermal_field)
        ext_a = pad_sides(with_halo_padding[:3], "constant")
        current_adjoint_vector = adj[3]
        floor_limit = jnp.where(
            leading_plane,
            jnp.where(entrance_face_flag == 1, jnp.float32(0.0), current_adjoint_vector[0]),
            with_halo_padding[3, 0],
        )
        ceiling_bound = jnp.where(
            trailing_plane, current_adjoint_vector[-1], with_halo_padding[3, -1]
        )
        ext_b = pad_sides(
            jnp.concatenate(
                [floor_limit[None], current_adjoint_vector, ceiling_bound[None]], axis=0
            ),
            "edge",
        )
        return adjoint_update(
            adj,
            ext_a,
            ext_b,
            padded_thermal_field,
            speed,
            alpha,
            porosity_sensitivity,
            solid,
            quadrature_factor,
        )

    grid_shape = (4,) + control_porosity.shape
    adj = jnp.zeros(grid_shape, jnp.float32)
    for interior_block in range(device_instant_total - 1, -1, -1):
        adj, unused = one_step(adj, interior_block)
    adj = passed_along(adj, "arc", -1)
    partial_sum = jnp.zeros(control_porosity.shape, jnp.float32)
    for interior_block in range(device_instant_total - 1, -1, -1):
        adj, summand_contribution = one_step(adj, interior_block)
        partial_sum = partial_sum + summand_contribution
    summed = lax.psum(partial_sum, "arc")
    share = summed.shape[1] // lax.axis_size("arc")
    gradient = lax.dynamic_slice_in_dim(summed, lax.axis_index("arc") * share, share, 1)
    return (gradient, adj[None])


def swap_over(value, partner_bit):
    count = lax.axis_size("space")
    return lax.ppermute(value, "space", [(i, i ^ partner_bit) for i in range(count)])


def in_space_order(me, axis, own, near, far, relay):
    pieces = [own, near, far, relay]
    odd = (me & 1) == 1
    pieces = [
        jnp.where(odd, pieces[1], pieces[0]),
        jnp.where(odd, pieces[0], pieces[1]),
        jnp.where(odd, pieces[3], pieces[2]),
        jnp.where(odd, pieces[2], pieces[3]),
    ]
    high = (me & 2) == 2
    pieces = [
        jnp.where(high, pieces[2], pieces[0]),
        jnp.where(high, pieces[3], pieces[1]),
        jnp.where(high, pieces[0], pieces[2]),
        jnp.where(high, pieces[1], pieces[3]),
    ]
    return jnp.concatenate(pieces, axis=axis)


def gathered_cells(local, me, axis):
    near = swap_over(local, 1)
    far = swap_over(local, 2)
    relay = swap_over(far, 1)
    return in_space_order(me, axis, local, near, far, relay)


def _shifted(f, axis, edge):
    n = f.shape[axis]
    idx = lax.broadcasted_iota(jnp.int32, f.shape, axis)
    up = pltpu.roll(f, n - 1, axis)
    down = pltpu.roll(f, 1, axis)
    up = jnp.where(idx == n - 1, f if edge else 0.0, up)
    down = jnp.where(idx == 0, f if edge else 0.0, down)
    return up, down


def _step_kernel(adj_ref, inp_ref, alpha_ref, solid_ref, ent_ref, out_ref):
    cells = adj_ref.shape[1]
    floor = ent_ref[...]
    for i in range(cells):
        lo = max(i - 1, 0)
        hi = min(i + 1, cells - 1)
        u = [inp_ref[d, i].astype(jnp.float32) for d in range(3)]
        t = inp_ref[3, i].astype(jnp.float32)
        t_hi = inp_ref[3, hi].astype(jnp.float32)
        t_lo = inp_ref[3, lo].astype(jnp.float32)
        t_r = _shifted(t, 0, True)
        t_l = _shifted(t, 1, True)
        grad_t = (0.5 * (t_hi - t_lo), 0.5 * (t_r[0] - t_r[1]), 0.5 * (t_l[0] - t_l[1]))
        b = adj_ref[3, i]
        b_hi = adj_ref[3, hi]
        if i == 0:
            b_lo = jnp.where(floor == 1.0, 0.0, b)
        else:
            b_lo = adj_ref[3, lo]
        alpha = alpha_ref[i]
        solid = solid_ref[i]
        for c in range(3):
            a = adj_ref[c, i]
            a_hi = adj_ref[c, hi] if i + 1 < cells else jnp.zeros_like(a)
            a_lo = adj_ref[c, lo] if i > 0 else jnp.zeros_like(a)
            a_r = _shifted(a, 0, False)
            a_l = _shifted(a, 1, False)
            lap = (a_hi + a_lo) + a_r[0] + a_r[1] + a_l[0] + a_l[1] - 6.0 * a
            carry = (
                u[0] * (0.5 * (a_hi - a_lo))
                + u[1] * (0.5 * (a_r[0] - a_r[1]))
                + u[2] * (0.5 * (a_l[0] - a_l[1]))
            )
            out_ref[c, i] = a + 0.1 * (1.2 * lap + carry - alpha * a - b * grad_t[c])
        b_r = _shifted(b, 0, True)
        b_l = _shifted(b, 1, True)
        lap_b = (b_hi + b_lo) + b_r[0] + b_r[1] + b_l[0] + b_l[1] - 6.0 * b
        carry_b = (
            u[0] * (0.5 * (b_hi - b_lo))
            + u[1] * (0.5 * (b_r[0] - b_r[1]))
            + u[2] * (0.5 * (b_l[0] - b_l[1]))
        )
        out_ref[3, i] = b + 0.1 * (1.2 * lap_b + carry_b - 2.0 * solid * b + 2.0 * solid)


def kernel_step(adj, inputs, alpha, solid, floor):
    vmem = pl.BlockSpec(memory_space=pltpu.VMEM)
    n = adj.size
    return pl.pallas_call(
        _step_kernel,
        out_shape=jax.ShapeDtypeStruct(adj.shape, adj.dtype),
        in_specs=[vmem] * 5,
        out_specs=vmem,
        cost_estimate=pl.CostEstimate(flops=40 * n, bytes_accessed=12 * n, transcendentals=0),
    )(adj, inputs, alpha, solid, floor)


def whole_grid_body(
    saved_velocity_trajectory,
    saved_warmth_trajectory,
    control_porosity,
    control_volume_flag,
    entrance_face_flag,
):
    lanes = saved_warmth_trajectory.shape[1]
    steps = saved_warmth_trajectory.shape[0]
    me = lax.axis_index("space")

    stacked = jnp.concatenate(
        [saved_velocity_trajectory, saved_warmth_trajectory[:, None]], axis=1
    )
    inputs_all = [None] * steps
    chunk = 2 if steps % 2 == 0 else 1
    near_all = swap_over(stacked, 1)
    for top in range(steps, 0, -chunk):
        own = stacked[top - chunk:top]
        far = swap_over(own, 2)
        relay = swap_over(far, 1)
        piece = in_space_order(me, 2, own, near_all[top - chunk:top], far, relay)
        for j in range(chunk):
            inputs_all[top - chunk + j] = piece[j]

    own_gamma = jnp.where(control_volume_flag == 1, control_porosity, jnp.float32(0.0))
    gamma = gathered_cells(own_gamma, me, 0)
    solid = 1.0 - gamma
    alpha = 3.0 * 0.1 * solid / (0.1 + gamma)
    own_flag = control_volume_flag.astype(jnp.float32)
    own_sensitivity = -3.0 * 0.1 * 1.1 / ((0.1 + own_gamma) * (0.1 + own_gamma))

    floor = entrance_face_flag.astype(jnp.float32)

    def one_step(adj, s):
        return kernel_step(adj, inputs_all[s], alpha, solid, floor)

    def own_cells(x, axis):
        return lax.dynamic_slice_in_dim(x, me * lanes, lanes, axis)

    def sensitivity(adj, s):
        a_loc = own_cells(adj[:3], 1)
        b_loc = own_cells(adj[3], 0)
        speed = saved_velocity_trajectory[s].astype(jnp.float32)
        thermal = saved_warmth_trajectory[s].astype(jnp.float32)
        dot = jnp.sum(a_loc * speed, axis=0)
        return 0.1 * own_flag * (own_sensitivity * dot + 2.0 * (b_loc - 1.0) * thermal)

    grid_shape = (4,) + gamma.shape
    adj = jnp.zeros(grid_shape, jnp.float32)
    for s in range(steps - 1, -1, -1):
        adj = one_step(adj, s)

    core = me % 2
    half = adj.shape[0] // 2
    mine = lax.dynamic_slice_in_dim(adj, core * half, half, 0)
    arrived = passed_along(mine, "arc", -1)
    space_count = lax.axis_size("space")
    swap = [(i, i ^ 1) for i in range(space_count)]
    other = lax.ppermute(arrived, "space", swap)
    adj = jnp.where(
        core == 0,
        jnp.concatenate([arrived, other], axis=0),
        jnp.concatenate([other, arrived], axis=0),
    )

    partial_sum = jnp.zeros(control_porosity.shape, jnp.float32)
    for s in range(steps - 1, -1, -1):
        partial_sum = partial_sum + sensitivity(adj, s)
        adj = one_step(adj, s)

    arcs = lax.axis_size("arc")
    k = lax.axis_index("arc")
    share = partial_sum.shape[1] // arcs
    pieces = partial_sum.reshape(partial_sum.shape[0], arcs, share, partial_sum.shape[2])
    total = lax.dynamic_index_in_dim(pieces, k, 1, keepdims=False)
    for shift in range(1, arcs):
        piece = lax.dynamic_index_in_dim(pieces, (k + shift) % arcs, 1, keepdims=False)
        total = total + passed_along(piece, "arc", shift)
    entry = own_cells(adj, 1)
    return (total, entry[None])


def solution(mesh):
    chosen = whole_grid_body if mesh.shape["space"] == 4 else halo_body
    return jax.shard_map(
        chosen,
        mesh=mesh,
        in_specs=(
            P(("job", "arc"), None, "space", None, None),
            P(("job", "arc"), "space", None, None),
            P(("job", "space"), None, None),
            P(("job", "space"), None, None),
            P("job", None),
        ),
        out_specs=(P(("job", "space"), "arc", None), P(("job", "arc"), None, "space", None, None)),
        check_vma=False,
    )
```

profile of v0, /device:TPU:0, one launch (start us, length us, event | category | flops | bytes accessed | tf_op | source)
XLA Modules:
  0.0 227.6 jit_solution(11485032618327472001)
XLA Ops:
  0.7 3.2 %pad_maximum_fusion = bf16[8,4,2,128,128]{4,3,2,1,0:T(8,128)(2,1)} fusion(bf16[8,1,2,128,128]{4,3,2,1,0:T(8,128)(2,1)} %bitcast.102, bf16[8,3,2,128,128]{4,3,2,1,0:T(8,128)(2,1)} %param.5), kind=kLoop, calls=%fused_computation.4 | loop fusion | flops 1048576 | bytes 4194304 | tf_op jit(solution)/shard_map/concatenate | solution.py:279
  3.9 0.5 collective-permute-start.2
  4.4 0.2 fusion.3
  4.6 2.6 %collective-permute-start.10 = (bf16[2,4,2,128,128]{4,3,2,1,0:T(8,128)(2,1)S(1)}, bf16[2,4,2,128,128]{4,3,2,1,0:T(8,128)(2,1)}, u32[]{:S(2)}, u32[]{:S(2)}) collective-permute-start(bf16[2,4,2,128,128]{4,3,2,1,0:T(8,128)(2,1)S(1)} %get-tuple-element.32), channel_id=1, source_target_pairs={{0,8},{4,12},{8,0},{12,4},{1,9},{5,13},{9,1},{13,5},{2,10},{6,14},... | collective-permute-start | bytes 1572872 | tf_op jit(solution)/shard_map/ppermute | solution.py:172
  7.2 0.1 collective-permute-start.6
  7.3 2.0 collective-permute-start.3
  9.3 24.5 %collective-permute-done.3 = f32[2,128,128]{2,1,0:T(8,128)S(1)} collective-permute-done((f32[2,128,128]{2,1,0:T(8,128)S(1)}, f32[2,128,128]{2,1,0:T(8,128)S(1)}, u32[]{:S(2)}, u32[]{:S(2)}) %collective-permute-start.3) | collective-permute-done | bytes 131104 | tf_op jit(solution)/shard_map/ppermute | solution.py:172
  33.8 1.8 collective-permute-start.8
  35.7 1.3 collective-permute-start
  37.0 0.5 collective-permute-start.7
  37.4 1.5 convert_element_type.87.ent_ref
  38.9 1.1 broadcast_select_fusion.39
  40.0 1.1 fusion.12
  41.1 7.7 %collective-permute-done.8 = bf16[2,4,2,128,128]{4,3,2,1,0:T(8,128)(2,1)} collective-permute-done((bf16[2,4,2,128,128]{4,3,2,1,0:T(8,128)(2,1)S(1)}, bf16[2,4,2,128,128]{4,3,2,1,0:T(8,128)(2,1)}, u32[]{:S(2)}, u32[]{:S(2)}) %collective-permute-start.8) | collective-permute-done | bytes 524320 | tf_op jit(solution)/shard_map/ppermute | solution.py:172
  48.8 10.7 %collective-permute-done = bf16[2,4,2,128,128]{4,3,2,1,0:T(8,128)(2,1)} collective-permute-done((bf16[2,4,2,128,128]{4,3,2,1,0:T(8,128)(2,1)S(1)}, bf16[2,4,2,128,128]{4,3,2,1,0:T(8,128)(2,1)}, u32[]{:S(2)}, u32[]{:S(2)}) %collective-permute-start) | collective-permute-done | bytes 524320 | tf_op jit(solution)/shard_map/ppermute | solution.py:172
  59.6 1.9 broadcast_select_fusion.19
  61.4 0.6 pad_maximum_fusion.2
  62.0 1.6 slice_bitcast_fusion.4
  63.6 1.6 broadcast_select_fusion.23
  65.2 1.0 pad_maximum_fusion.1
  66.3 1.6 slice_bitcast_fusion.6
  67.8 1.6 slice_bitcast_fusion.2
  69.4 1.6 slice_bitcast_fusion
  71.0 1.6 broadcast_in_dim.14.adj_ref
  72.5 6.1 %shard_map.68.adj_ref = f32[4,8,128,128]{3,2,1,0:T(8,128)} custom-call(f32[4,8,128,128]{3,2,1,0:T(8,128)} %broadcast_in_dim.14.adj_ref, bf16[4,8,128,128]{3,2,1,0:T(8,128)(2,1)} %get-tuple-element.45.inp_ref, f32[8,128,128]{2,1,0:T(8,128)} %get-tuple-element.47.alpha_ref, f32[8,128,128]{2,1,0:T(8,128)} %get-tuple-element.46.solid_ref, ...), custom_call_target="tpu_custom_call" | custom-call | flops 20971520 | bytes 6291456 | tf_op jit(solution)/shard_map/pallas_call | solution.py:259
  78.6 6.1 %shard_map.69.adj_ref = f32[4,8,128,128]{3,2,1,0:T(8,128)} custom-call(f32[4,8,128,128]{3,2,1,0:T(8,128)} %shard_map.68.adj_ref, bf16[4,8,128,128]{3,2,1,0:T(8,128)(2,1)} %get-tuple-element.44.inp_ref, f32[8,128,128]{2,1,0:T(8,128)} %get-tuple-element.47.alpha_ref, f32[8,128,128]{2,1,0:T(8,128)} %get-tuple-element.46.solid_ref, ...), custom_call_target="tpu_custom_call" | custom-call | flops 20971520 | bytes 6291456 | tf_op jit(solution)/shard_map/pallas_call | solution.py:259
  84.7 6.1 %shard_map.70.adj_ref = f32[4,8,128,128]{3,2,1,0:T(8,128)} custom-call(f32[4,8,128,128]{3,2,1,0:T(8,128)} %shard_map.69.adj_ref, bf16[4,8,128,128]{3,2,1,0:T(8,128)(2,1)} %get-tuple-element.43.inp_ref, f32[8,128,128]{2,1,0:T(8,128)} %get-tuple-element.47.alpha_ref, f32[8,128,128]{2,1,0:T(8,128)} %get-tuple-element.46.solid_ref, ...), custom_call_target="tpu_custom_call" | custom-call | flops 20971520 | bytes 6291456 | tf_op jit(solution)/shard_map/pallas_call | solution.py:259
  90.8 6.1 %shard_map.71.adj_ref = f32[4,8,128,128]{3,2,1,0:T(8,128)} custom-call(f32[4,8,128,128]{3,2,1,0:T(8,128)} %shard_map.70.adj_ref, bf16[4,8,128,128]{3,2,1,0:T(8,128)(2,1)} %get-tuple-element.42.inp_ref, f32[8,128,128]{2,1,0:T(8,128)} %get-tuple-element.47.alpha_ref, f32[8,128,128]{2,1,0:T(8,128)} %get-tuple-element.46.solid_ref, ...), custom_call_target="tpu_custom_call" | custom-call | flops 20971520 | bytes 6291456 | tf_op jit(solution)/shard_map/pallas_call | solution.py:259
  96.8 6.2 %shard_map.72.adj_ref = f32[4,8,128,128]{3,2,1,0:T(8,128)} custom-call(f32[4,8,128,128]{3,2,1,0:T(8,128)} %shard_map.71.adj_ref, bf16[4,8,128,128]{3,2,1,0:T(8,128)(2,1)} %get-tuple-element.37.inp_ref, f32[8,128,128]{2,1,0:T(8,128)} %get-tuple-element.47.alpha_ref, f32[8,128,128]{2,1,0:T(8,128)} %get-tuple-element.46.solid_ref, ...), custom_call_target="tpu_custom_call" | custom-call | flops 20971520 | bytes 6291456 | tf_op jit(solution)/shard_map/pallas_call | solution.py:259
  103.1 6.1 %shard_map.73.adj_ref = f32[4,8,128,128]{3,2,1,0:T(8,128)} custom-call(f32[4,8,128,128]{3,2,1,0:T(8,128)} %shard_map.72.adj_ref, bf16[4,8,128,128]{3,2,1,0:T(8,128)(2,1)} %get-tuple-element.36.inp_ref, f32[8,128,128]{2,1,0:T(8,128)} %get-tuple-element.47.alpha_ref, f32[8,128,128]{2,1,0:T(8,128)} %get-tuple-element.46.solid_ref, ...), custom_call_target="tpu_custom_call" | custom-call | flops 20971520 | bytes 6291456 | tf_op jit(solution)/shard_map/pallas_call | solution.py:259
  109.1 6.1 %shard_map.74.adj_ref = f32[4,8,128,128]{3,2,1,0:T(8,128)} custom-call(f32[4,8,128,128]{3,2,1,0:T(8,128)} %shard_map.73.adj_ref, bf16[4,8,128,128]{3,2,1,0:T(8,128)(2,1)} %get-tuple-element.27.inp_ref, f32[8,128,128]{2,1,0:T(8,128)} %get-tuple-element.47.alpha_ref, f32[8,128,128]{2,1,0:T(8,128)} %get-tuple-element.46.solid_ref, ...), custom_call_target="tpu_custom_call" | custom-call | flops 20971520 | bytes 6291456 | tf_op jit(solution)/shard_map/pallas_call | solution.py:259
  115.2 6.1 %shard_map.75 = f32[4,8,128,128]{3,2,1,0:T(8,128)} custom-call(f32[4,8,128,128]{3,2,1,0:T(8,128)} %shard_map.74.adj_ref, bf16[4,8,128,128]{3,2,1,0:T(8,128)(2,1)} %get-tuple-element.26.inp_ref, f32[8,128,128]{2,1,0:T(8,128)} %get-tuple-element.47.alpha_ref, f32[8,128,128]{2,1,0:T(8,128)} %get-tuple-element.46.solid_ref, f32[128,128]{1,0:T(8,128)} %convert_element_type.87.ent_ref), custom_call_target="tpu_custom_call" | custom-call | flops 20971520 | bytes 6291456 | tf_op jit(solution)/shard_map/pallas_call | solution.py:259
  121.3 1.3 constant_dynamic-slice_fusion
  122.6 4.1 %collective-permute-start.12 = (f32[2,8,128,128]{3,2,1,0:T(8,128)S(1)}, f32[2,8,128,128]{3,2,1,0:T(8,128)S(1)}, u32[]{:S(2)}, u32[]{:S(2)}) collective-permute-start(f32[2,8,128,128]{3,2,1,0:T(8,128)S(1)} %constant_dynamic-slice_fusion), channel_id=1, source_target_pairs={{0,3},{1,0},{2,1},{3,2},{4,7},{5,4},{6,5},{7,6},{8,11},{9,8},{10,9... | collective-permute-start | bytes 3145736 | tf_op jit(solution)/shard_map/ppermute | solution.py:29
  126.7 23.1 %collective-permute-done.12 = f32[2,8,128,128]{3,2,1,0:T(8,128)S(1)} collective-permute-done((f32[2,8,128,128]{3,2,1,0:T(8,128)S(1)}, f32[2,8,128,128]{3,2,1,0:T(8,128)S(1)}, u32[]{:S(2)}, u32[]{:S(2)}) %collective-permute-start.12) | collective-permute-done | bytes 1048608 | tf_op jit(solution)/shard_map/ppermute | solution.py:29
  149.8 2.8 %collective-permute-done.13 = f32[2,8,128,128]{3,2,1,0:T(8,128)} collective-permute-done((f32[2,8,128,128]{3,2,1,0:T(8,128)S(1)}, f32[2,8,128,128]{3,2,1,0:T(8,128)}, u32[]{:S(2)}, u32[]{:S(2)}) %collective-permute-start.13) | collective-permute-done | bytes 1048608 | tf_op jit(solution)/shard_map/ppermute | solution.py:327
  152.6 1.8 maximum_select_fusion.adj_ref
  154.3 1.3 copy-done.3
  155.7 6.1 %shard_map.76.adj_ref = f32[4,8,128,128]{3,2,1,0:T(8,128)} custom-call(f32[4,8,128,128]{3,2,1,0:T(8,128)} %copy-done.3, bf16[4,8,128,128]{3,2,1,0:T(8,128)(2,1)} %get-tuple-element.45.inp_ref, f32[8,128,128]{2,1,0:T(8,128)} %get-tuple-element.47.alpha_ref, f32[8,128,128]{2,1,0:T(8,128)} %get-tuple-element.46.solid_ref, f32[128,128]{1,0:T(8,128)} %convert_element_type.87.ent_ref), custom_call_target="tpu_custom_call" | custom-call | flops 20971520 | bytes 6291456 | tf_op jit(solution)/shard_map/pallas_call | solution.py:259
  161.8 2.7 %slice.212 = f32[3,8,128,128]{3,2,1,0:T(8,128)} slice(f32[4,8,128,128]{3,2,1,0:T(8,128)} %copy-done.3), slice={[0:3], [0:8], [0:128], [0:128]} | slice | bytes 3145728 | tf_op jit(solution)/shard_map/slice | solution.py:309
  164.5 6.1 %shard_map.77.adj_ref = f32[4,8,128,128]{3,2,1,0:T(8,128)} custom-call(f32[4,8,128,128]{3,2,1,0:T(8,128)} %shard_map.76.adj_ref, bf16[4,8,128,128]{3,2,1,0:T(8,128)(2,1)} %get-tuple-element.44.inp_ref, f32[8,128,128]{2,1,0:T(8,128)} %get-tuple-element.47.alpha_ref, f32[8,128,128]{2,1,0:T(8,128)} %get-tuple-element.46.solid_ref, ...), custom_call_target="tpu_custom_call" | custom-call | flops 20971520 | bytes 6291456 | tf_op jit(solution)/shard_map/pallas_call | solution.py:259
  170.6 6.2 %shard_map.78.adj_ref = f32[4,8,128,128]{3,2,1,0:T(8,128)} custom-call(f32[4,8,128,128]{3,2,1,0:T(8,128)} %shard_map.77.adj_ref, bf16[4,8,128,128]{3,2,1,0:T(8,128)(2,1)} %get-tuple-element.43.inp_ref, f32[8,128,128]{2,1,0:T(8,128)} %get-tuple-element.47.alpha_ref, f32[8,128,128]{2,1,0:T(8,128)} %get-tuple-element.46.solid_ref, ...), custom_call_target="tpu_custom_call" | custom-call | flops 20971520 | bytes 6291456 | tf_op jit(solution)/shard_map/pallas_call | solution.py:259
  176.8 6.1 %shard_map.79.adj_ref = f32[4,8,128,128]{3,2,1,0:T(8,128)} custom-call(f32[4,8,128,128]{3,2,1,0:T(8,128)} %shard_map.78.adj_ref, bf16[4,8,128,128]{3,2,1,0:T(8,128)(2,1)} %get-tuple-element.42.inp_ref, f32[8,128,128]{2,1,0:T(8,128)} %get-tuple-element.47.alpha_ref, f32[8,128,128]{2,1,0:T(8,128)} %get-tuple-element.46.solid_ref, ...), custom_call_target="tpu_custom_call" | custom-call | flops 20971520 | bytes 6291456 | tf_op jit(solution)/shard_map/pallas_call | solution.py:259
  182.8 6.5 %shard_map.80.adj_ref = f32[4,8,128,128]{3,2,1,0:T(8,128)} custom-call(f32[4,8,128,128]{3,2,1,0:T(8,128)} %shard_map.79.adj_ref, bf16[4,8,128,128]{3,2,1,0:T(8,128)(2,1)} %get-tuple-element.37.inp_ref, f32[8,128,128]{2,1,0:T(8,128)} %get-tuple-element.47.alpha_ref, f32[8,128,128]{2,1,0:T(8,128)} %get-tuple-element.46.solid_ref, ...), custom_call_target="tpu_custom_call" | custom-call | flops 20971520 | bytes 6291456 | tf_op jit(solution)/shard_map/pallas_call | solution.py:259
  189.3 1.3 slice.220
  190.6 6.2 %shard_map.81.adj_ref = f32[4,8,128,128]{3,2,1,0:T(8,128)} custom-call(f32[4,8,128,128]{3,2,1,0:T(8,128)} %shard_map.80.adj_ref, bf16[4,8,128,128]{3,2,1,0:T(8,128)(2,1)} %get-tuple-element.36.inp_ref, f32[8,128,128]{2,1,0:T(8,128)} %get-tuple-element.47.alpha_ref, f32[8,128,128]{2,1,0:T(8,128)} %get-tuple-element.46.solid_ref, ...), custom_call_target="tpu_custom_call" | custom-call | flops 20971520 | bytes 6291456 | tf_op jit(solution)/shard_map/pallas_call | solution.py:259
  196.8 1.3 slice.222
  198.1 6.2 %shard_map.82.adj_ref = f32[4,8,128,128]{3,2,1,0:T(8,128)} custom-call(f32[4,8,128,128]{3,2,1,0:T(8,128)} %shard_map.81.adj_ref, bf16[4,8,128,128]{3,2,1,0:T(8,128)(2,1)} %get-tuple-element.27.inp_ref, f32[8,128,128]{2,1,0:T(8,128)} %get-tuple-element.47.alpha_ref, f32[8,128,128]{2,1,0:T(8,128)} %get-tuple-element.46.solid_ref, ...), custom_call_target="tpu_custom_call" | custom-call | flops 20971520 | bytes 6291456 | tf_op jit(solution)/shard_map/pallas_call | solution.py:259
  204.3 1.3 slice.224
  205.7 6.2 %shard_map.83 = f32[4,8,128,128]{3,2,1,0:T(8,128)} custom-call(f32[4,8,128,128]{3,2,1,0:T(8,128)} %shard_map.82.adj_ref, bf16[4,8,128,128]{3,2,1,0:T(8,128)(2,1)} %get-tuple-element.26.inp_ref, f32[8,128,128]{2,1,0:T(8,128)} %get-tuple-element.47.alpha_ref, f32[8,128,128]{2,1,0:T(8,128)} %get-tuple-element.46.solid_ref, f32[128,128]{1,0:T(8,128)} %convert_element_type.87.ent_ref), custom_call_target="tpu_custom_call" | custom-call | flops 20971520 | bytes 6291456 | tf_op jit(solution)/shard_map/pallas_call | solution.py:259
  211.8 1.4 slice-done.1
  213.2 0.5 slice-done.3
  213.8 2.7 %fusion.11 = (f32[2,128,128]{2,1,0:T(8,128)S(1)}, f32[2,128,128]{2,1,0:T(8,128)S(1)}, f32[2,128,128]{2,1,0:T(8,128)S(1)}, f32[2,128,128]{2,1,0:T(8,128)S(1)}, f3...) fusion(f32[3,8,128,128]{3,2,1,0:T(8,128)} %slice.212, ...), kind=kLoop, calls=%fused_computation.76 | loop fusion | flops 2097152 | bytes 5767172 | tf_op jit(solution)/shard_map/reduce_sum | solution.py:313
  216.5 0.0 slice-done.9
  216.5 0.2 slice-done.10
  216.7 0.2 slice-done.11
  216.8 0.2 copy-done.6
  217.0 0.3 fusion.14
  217.3 0.5 collective-permute-start.14
  217.8 3.9 %collective-permute-start.16 = (f32[2,32,128]{2,1,0:T(8,128)S(1)}, f32[2,32,128]{2,1,0:T(8,128)S(1)}, u32[]{:S(2)}, u32[]{:S(2)}) collective-permute-start(f32[2,32,128]{2,1,0:T(8,128)S(1)} %get-tuple-element.53), channel_id=1, source_target_pairs={{0,3},{1,0},{2,1},{3,2},{4,7},{5,4},{6,5},{7,6},{8,11},{9,8},{10,9... | collective-permute-start | bytes 98312 | tf_op jit(solution)/shard_map/ppermute | solution.py:29
  221.7 0.5 collective-permute-start.15
  222.2 1.9 dynamic-slice_bitcast_fusion
  224.1 2.4 %collective-permute-done.15 = f32[2,32,128]{2,1,0:T(8,128)S(1)} collective-permute-done((f32[2,32,128]{2,1,0:T(8,128)S(1)}, f32[2,32,128]{2,1,0:T(8,128)S(1)}, u32[]{:S(2)}, u32[]{:S(2)}) %collective-permute-start.15) | collective-permute-done | bytes 32800 | tf_op jit(solution)/shard_map/ppermute | solution.py:29
  226.5 0.6 fusion.22
  (66 shorter events, 0.2 us)
Async XLA Ops:
  0.6 3.8 %copy-start.4 = (bf16[8,3,2,128,128]{4,3,2,1,0:T(8,128)(2,1)S(1)}, bf16[8,3,2,128,128]{4,3,2,1,0:T(8,128)(2,1)}, u32[]{:S(2)}) copy-start(bf16[8,3,2,128,128]{4,3,2,1,0:T(8,128)(2,1)} %param.5) | copy-start | bytes 4718596
  0.6 3.8 %copy-start.5 = (bf16[8,2,128,128]{3,2,1,0:T(8,128)(2,1)S(1)}, bf16[8,2,128,128]{3,2,1,0:T(8,128)(2,1)}, u32[]{:S(2)}) copy-start(bf16[8,2,128,128]{3,2,1,0:T(8,128)(2,1)} %param.6) | copy-start | bytes 1572868
  3.9 3.4 %copy-start.11 = (s32[2,128,128]{2,1,0:T(8,128)S(1)}, s32[2,128,128]{2,1,0:T(8,128)}, u32[]{:S(2)}) copy-start(s32[2,128,128]{2,1,0:T(8,128)} %param.8) | copy-start | bytes 393220
  3.9 3.4 %copy-start.12 = (f32[2,128,128]{2,1,0:T(8,128)S(1)}, f32[2,128,128]{2,1,0:T(8,128)}, u32[]{:S(2)}) copy-start(f32[2,128,128]{2,1,0:T(8,128)} %param.7) | copy-start | bytes 393220
  3.9 55.6 %collective-permute-start.2 = (bf16[8,4,2,128,128]{4,3,2,1,0:T(8,128)(2,1)}, bf16[8,4,2,128,128]{4,3,2,1,0:T(8,128)(2,1)S(1)}, u32[]{:S(2)}, u32[]{:S(2)}) collective-permute-start(bf16[8,4,2,128,128]{4,3,2,1,0:T(8,128)(2,1)} %pad_maximum_fusion), channel_id=1, source_target_pairs={{0,4},{4,0},{8,12},{12,8},{1,5},{5,1},{9,13},{13,9},{2,6},{6,2},{1... | collective-permute-start | bytes 6291464 | tf_op jit(solution)/shard_map/ppermute | solution.py:172
  4.6 31.1 %copy-start.7 = (bf16[2,4,2,128,128]{4,3,2,1,0:T(8,128)(2,1)}, bf16[2,4,2,128,128]{4,3,2,1,0:T(8,128)(2,1)S(1)}, u32[]{:S(2)}) copy-start(bf16[2,4,2,128,128]{4,3,2,1,0:T(8,128)(2,1)S(1)} %get-tuple-element.32) | copy-start | bytes 1572868
  4.6 32.3 %copy-start.9 = (bf16[2,4,2,128,128]{4,3,2,1,0:T(8,128)(2,1)}, bf16[2,4,2,128,128]{4,3,2,1,0:T(8,128)(2,1)S(1)}, u32[]{:S(2)}) copy-start(bf16[2,4,2,128,128]{4,3,2,1,0:T(8,128)(2,1)S(1)} %get-tuple-element.34) | copy-start | bytes 1572868
  4.6 32.3 %collective-permute-start.10 = (bf16[2,4,2,128,128]{4,3,2,1,0:T(8,128)(2,1)S(1)}, bf16[2,4,2,128,128]{4,3,2,1,0:T(8,128)(2,1)}, u32[]{:S(2)}, u32[]{:S(2)}) collective-permute-start(bf16[2,4,2,128,128]{4,3,2,1,0:T(8,128)(2,1)S(1)} %get-tuple-element.32), channel_id=1, source_target_pairs={{0,8},{4,12},{8,0},{12,4},{1,9},{5,13},{9,1},{13,5},{2,10},{6,14},... | collective-permute-start | bytes 1572872 | tf_op jit(solution)/shard_map/ppermute | solution.py:172
  7.2 29.7 %collective-permute-start.6 = (bf16[2,4,2,128,128]{4,3,2,1,0:T(8,128)(2,1)S(1)}, bf16[2,4,2,128,128]{4,3,2,1,0:T(8,128)(2,1)}, u32[]{:S(2)}, u32[]{:S(2)}) collective-permute-start(bf16[2,4,2,128,128]{4,3,2,1,0:T(8,128)(2,1)S(1)} %get-tuple-element.34), channel_id=1, source_target_pairs={{0,8},{4,12},{8,0},{12,4},{1,9},{5,13},{9,1},{13,5},{2,10},{6,14},... | collective-permute-start | bytes 1572872 | tf_op jit(solution)/shard_map/ppermute | solution.py:172
  7.3 26.5 %collective-permute-start.3 = (f32[2,128,128]{2,1,0:T(8,128)S(1)}, f32[2,128,128]{2,1,0:T(8,128)S(1)}, u32[]{:S(2)}, u32[]{:S(2)}) collective-permute-start(f32[2,128,128]{2,1,0:T(8,128)S(1)} %compare_select_fusion), channel_id=1, source_target_pairs={{0,8},{4,12},{8,0},{12,4},{1,9},{5,13},{9,1},{13,5},{2,10},{6,14},... | collective-permute-start | bytes 393224 | tf_op jit(solution)/shard_map/ppermute | solution.py:172
  9.3 24.5 %collective-permute-start.5 = (f32[2,128,128]{2,1,0:T(8,128)S(1)}, f32[2,128,128]{2,1,0:T(8,128)S(1)}, u32[]{:S(2)}, u32[]{:S(2)}) collective-permute-start(f32[2,128,128]{2,1,0:T(8,128)S(1)} %compare_select_fusion), channel_id=1, source_target_pairs={{0,4},{4,0},{8,12},{12,8},{1,5},{5,1},{9,13},{13,9},{2,6},{6,2},{1... | collective-permute-start | bytes 393224 | tf_op jit(solution)/shard_map/ppermute | solution.py:172
  33.8 1.8 collective-permute-start.4
  33.8 3.1 %copy-start.13 = (f32[2,128,128]{2,1,0:T(8,128)}, f32[2,128,128]{2,1,0:T(8,128)S(1)}, u32[]{:S(2)}) copy-start(f32[2,128,128]{2,1,0:T(8,128)S(1)} %collective-permute-done.5) | copy-start | bytes 393220
  33.8 15.0 %collective-permute-start.8 = (bf16[2,4,2,128,128]{4,3,2,1,0:T(8,128)(2,1)S(1)}, bf16[2,4,2,128,128]{4,3,2,1,0:T(8,128)(2,1)}, u32[]{:S(2)}, u32[]{:S(2)}) collective-permute-start(bf16[2,4,2,128,128]{4,3,2,1,0:T(8,128)(2,1)S(1)} %get-tuple-element.33), channel_id=1, source_target_pairs={{0,8},{4,12},{8,0},{12,4},{1,9},{5,13},{9,1},{13,5},{2,10},{6,14},... | collective-permute-start | bytes 1572872 | tf_op jit(solution)/shard_map/ppermute | solution.py:172
  35.6 1.8 copy-start.14
  35.7 23.9 %collective-permute-start = (bf16[2,4,2,128,128]{4,3,2,1,0:T(8,128)(2,1)S(1)}, bf16[2,4,2,128,128]{4,3,2,1,0:T(8,128)(2,1)}, u32[]{:S(2)}, u32[]{:S(2)}) collective-permute-start(bf16[2,4,2,128,128]{4,3,2,1,0:T(8,128)(2,1)S(1)} %get-tuple-element.35), channel_id=1, source_target_pairs={{0,8},{4,12},{8,0},{12,4},{1,9},{5,13},{9,1},{13,5},{2,10},{6,14},... | collective-permute-start | bytes 1572872 | tf_op jit(solution)/shard_map/ppermute | solution.py:172
  36.9 22.6 %collective-permute-start.11 = (bf16[2,4,2,128,128]{4,3,2,1,0:T(8,128)(2,1)}, bf16[2,4,2,128,128]{4,3,2,1,0:T(8,128)(2,1)}, u32[]{:S(2)}, u32[]{:S(2)}) collective-permute-start(bf16[2,4,2,128,128]{4,3,2,1,0:T(8,128)(2,1)} %collective-permute-done.10), channel_id=1, source_target_pairs={{0,4},{4,0},{8,12},{12,8},{1,5},{5,1},{9,13},{13,9},{2,6},{6,2},{1... | collective-permute-start | bytes 1572872 | tf_op jit(solution)/shard_map/ppermute | solution.py:172
  37.0 22.6 %collective-permute-start.7 = (bf16[2,4,2,128,128]{4,3,2,1,0:T(8,128)(2,1)}, bf16[2,4,2,128,128]{4,3,2,1,0:T(8,128)(2,1)}, u32[]{:S(2)}, u32[]{:S(2)}) collective-permute-start(bf16[2,4,2,128,128]{4,3,2,1,0:T(8,128)(2,1)} %collective-permute-done.6), channel_id=1, source_target_pairs={{0,4},{4,0},{8,12},{12,8},{1,5},{5,1},{9,13},{13,9},{2,6},{6,2},{1... | collective-permute-start | bytes 1572872 | tf_op jit(solution)/shard_map/ppermute | solution.py:172
  38.9 20.6 %copy-start.8 = (bf16[2,4,2,128,128]{4,3,2,1,0:T(8,128)(2,1)S(1)}, bf16[2,4,2,128,128]{4,3,2,1,0:T(8,128)(2,1)}, u32[]{:S(2)}) copy-start(bf16[2,4,2,128,128]{4,3,2,1,0:T(8,128)(2,1)} %copy-done.7) | copy-start | bytes 1572868
  38.9 20.6 %copy-start.10 = (bf16[2,4,2,128,128]{4,3,2,1,0:T(8,128)(2,1)S(1)}, bf16[2,4,2,128,128]{4,3,2,1,0:T(8,128)(2,1)}, u32[]{:S(2)}) copy-start(bf16[2,4,2,128,128]{4,3,2,1,0:T(8,128)(2,1)} %copy-done.9) | copy-start | bytes 1572868
  48.8 14.8 %collective-permute-start.9 = (bf16[2,4,2,128,128]{4,3,2,1,0:T(8,128)(2,1)}, bf16[2,4,2,128,128]{4,3,2,1,0:T(8,128)(2,1)S(1)}, u32[]{:S(2)}, u32[]{:S(2)}) collective-permute-start(bf16[2,4,2,128,128]{4,3,2,1,0:T(8,128)(2,1)} %collective-permute-done.8), channel_id=1, source_target_pairs={{0,4},{4,0},{8,12},{12,8},{1,5},{5,1},{9,13},{13,9},{2,6},{6,2},{1... | collective-permute-start | bytes 1572872 | tf_op jit(solution)/shard_map/ppermute | solution.py:172
  59.5 4.1 %collective-permute-start.1 = (bf16[2,4,2,128,128]{4,3,2,1,0:T(8,128)(2,1)}, bf16[2,4,2,128,128]{4,3,2,1,0:T(8,128)(2,1)S(1)}, u32[]{:S(2)}, u32[]{:S(2)}) collective-permute-start(bf16[2,4,2,128,128]{4,3,2,1,0:T(8,128)(2,1)} %collective-permute-done), channel_id=1, source_target_pairs={{0,4},{4,0},{8,12},{12,8},{1,5},{5,1},{9,13},{13,9},{2,6},{6,2},{1... | collective-permute-start | bytes 1572872 | tf_op jit(solution)/shard_map/ppermute | solution.py:172
  122.6 27.2 %collective-permute-start.12 = (f32[2,8,128,128]{3,2,1,0:T(8,128)S(1)}, f32[2,8,128,128]{3,2,1,0:T(8,128)S(1)}, u32[]{:S(2)}, u32[]{:S(2)}) collective-permute-start(f32[2,8,128,128]{3,2,1,0:T(8,128)S(1)} %constant_dynamic-slice_fusion), channel_id=1, source_target_pairs={{0,3},{1,0},{2,1},{3,2},{4,7},{5,4},{6,5},{7,6},{8,11},{9,8},{10,9... | collective-permute-start | bytes 3145736 | tf_op jit(solution)/shard_map/ppermute | solution.py:29
  149.8 2.8 %collective-permute-start.13 = (f32[2,8,128,128]{3,2,1,0:T(8,128)S(1)}, f32[2,8,128,128]{3,2,1,0:T(8,128)}, u32[]{:S(2)}, u32[]{:S(2)}) collective-permute-start(f32[2,8,128,128]{3,2,1,0:T(8,128)S(1)} %collective-permute-done.12), channel_id=1, source_target_pairs={{0,4},{4,0},{8,12},{12,8},{1,5},{5,1},{9,13},{13,9},{2,6},{6,2},{1... | collective-permute-start | bytes 3145736 | tf_op jit(solution)/shard_map/ppermute | solution.py:327
  154.3 1.4 copy-start.3
  182.8 6.5 %copy-start = (f32[4,8,128,128]{3,2,1,0:T(8,128)S(1)}, f32[4,8,128,128]{3,2,1,0:T(8,128)}, u32[]{:S(2)}) copy-start(f32[4,8,128,128]{3,2,1,0:T(8,128)} %shard_map.79.adj_ref) | copy-start | bytes 6291460
  190.6 6.2 %copy-start.1 = (f32[4,8,128,128]{3,2,1,0:T(8,128)S(1)}, f32[4,8,128,128]{3,2,1,0:T(8,128)}, u32[]{:S(2)}) copy-start(f32[4,8,128,128]{3,2,1,0:T(8,128)} %shard_map.80.adj_ref) | copy-start | bytes 6291460
  198.1 6.2 %copy-start.2 = (f32[4,8,128,128]{3,2,1,0:T(8,128)S(1)}, f32[4,8,128,128]{3,2,1,0:T(8,128)}, u32[]{:S(2)}) copy-start(f32[4,8,128,128]{3,2,1,0:T(8,128)} %shard_map.81.adj_ref) | copy-start | bytes 6291460
  205.6 6.2 %slice-start.5 = ((f32[4,8,128,128]{3,2,1,0:T(8,128)}), f32[3,8,128,128]{3,2,1,0:T(8,128)S(1)}, s32[]{:S(2)}) async-start(f32[4,8,128,128]{3,2,1,0:T(8,128)} %shard_map.77.adj_ref), calls=%async_computation.5 | async-start | bytes 3145728 | tf_op jit(solution)/shard_map/slice | solution.py:309
  205.6 6.2 %slice-start.7 = ((f32[4,8,128,128]{3,2,1,0:T(8,128)}), f32[3,8,128,128]{3,2,1,0:T(8,128)S(1)}, s32[]{:S(2)}) async-start(f32[4,8,128,128]{3,2,1,0:T(8,128)} %shard_map.78.adj_ref), calls=%async_computation.7 | async-start | bytes 3145728 | tf_op jit(solution)/shard_map/slice | solution.py:309
  211.8 1.4 slice-start.1
  211.8 1.9 slice-start.3
  213.7 2.7 %slice-start = ((f32[4,8,128,128]{3,2,1,0:T(8,128)}), f32[1,8,128,128]{3,2,1,0:T(8,128)S(1)}, s32[]{:S(2)}) async-start(f32[4,8,128,128]{3,2,1,0:T(8,128)} %shard_map.82.adj_ref), calls=%async_computation | async-start | bytes 1048576 | tf_op jit(solution)/shard_map/slice | solution.py:310
  213.7 2.7 %slice-start.2 = ((f32[4,8,128,128]{3,2,1,0:T(8,128)}), f32[1,8,128,128]{3,2,1,0:T(8,128)S(1)}, s32[]{:S(2)}) async-start(f32[4,8,128,128]{3,2,1,0:T(8,128)} %shard_map.76.adj_ref), calls=%async_computation.2 | async-start | bytes 1048576 | tf_op jit(solution)/shard_map/slice | solution.py:310
  213.7 2.7 %slice-start.4 = ((f32[4,8,128,128]{3,2,1,0:T(8,128)}), f32[1,8,128,128]{3,2,1,0:T(8,128)S(1)}, s32[]{:S(2)}) async-start(f32[4,8,128,128]{3,2,1,0:T(8,128)} %shard_map.77.adj_ref), calls=%async_computation.4 | async-start | bytes 1048576 | tf_op jit(solution)/shard_map/slice | solution.py:310
  213.7 2.8 %slice-start.6 = ((f32[4,8,128,128]{3,2,1,0:T(8,128)}), f32[1,8,128,128]{3,2,1,0:T(8,128)S(1)}, s32[]{:S(2)}) async-start(f32[4,8,128,128]{3,2,1,0:T(8,128)} %shard_map.78.adj_ref), calls=%async_computation.6 | async-start | bytes 1048576 | tf_op jit(solution)/shard_map/slice | solution.py:310
  213.7 2.8 %slice-start.8 = ((f32[4,8,128,128]{3,2,1,0:T(8,128)}), f32[1,8,128,128]{3,2,1,0:T(8,128)S(1)}, s32[]{:S(2)}) async-start(f32[4,8,128,128]{3,2,1,0:T(8,128)} %shard_map.79.adj_ref), calls=%async_computation.8 | async-start | bytes 1048576 | tf_op jit(solution)/shard_map/slice | solution.py:310
  213.7 2.8 %slice-start.9 = ((f32[4,8,128,128]{3,2,1,0:T(8,128)}), f32[1,8,128,128]{3,2,1,0:T(8,128)S(1)}, s32[]{:S(2)}) async-start(f32[4,8,128,128]{3,2,1,0:T(8,128)} %shard_map.80.adj_ref), calls=%async_computation.9 | async-start | bytes 1048576 | tf_op jit(solution)/shard_map/slice | solution.py:310
  213.7 2.9 %slice-start.10 = ((f32[4,8,128,128]{3,2,1,0:T(8,128)}), f32[1,8,128,128]{3,2,1,0:T(8,128)S(1)}, s32[]{:S(2)}) async-start(f32[4,8,128,128]{3,2,1,0:T(8,128)} %shard_map.81.adj_ref), calls=%async_computation.10 | async-start | bytes 1048576 | tf_op jit(solution)/shard_map/slice | solution.py:310
  213.7 3.1 %slice-start.11 = ((f32[4,8,128,128]{3,2,1,0:T(8,128)}), f32[1,8,128,128]{3,2,1,0:T(8,128)S(1)}, s32[]{:S(2)}) async-start(f32[4,8,128,128]{3,2,1,0:T(8,128)} %copy-done.3), calls=%async_computation.11 | async-start | bytes 1048576 | tf_op jit(solution)/shard_map/slice | solution.py:310
  213.8 3.2 %copy-start.6 = (bf16[8,2,128,128]{3,2,1,0:T(8,128)(2,1)S(1)}, bf16[8,2,128,128]{3,2,1,0:T(8,128)(2,1)}, u32[]{:S(2)}) copy-start(bf16[8,2,128,128]{3,2,1,0:T(8,128)(2,1)} %param.6) | copy-start | bytes 1572868
  217.3 6.8 %collective-permute-start.14 = (f32[2,32,128]{2,1,0:T(8,128)S(1)}, f32[2,32,128]{2,1,0:T(8,128)S(1)}, u32[]{:S(2)}, u32[]{:S(2)}) collective-permute-start(f32[2,32,128]{2,1,0:T(8,128)S(1)} %get-tuple-element.52), channel_id=1, source_target_pairs={{0,1},{1,2},{2,3},{3,0},{4,5},{5,6},{6,7},{7,4},{8,9},{9,10},{10,1... | collective-permute-start | bytes 98312 | tf_op jit(solution)/shard_map/ppermute | solution.py:29
  217.8 6.3 %collective-permute-start.16 = (f32[2,32,128]{2,1,0:T(8,128)S(1)}, f32[2,32,128]{2,1,0:T(8,128)S(1)}, u32[]{:S(2)}, u32[]{:S(2)}) collective-permute-start(f32[2,32,128]{2,1,0:T(8,128)S(1)} %get-tuple-element.53), channel_id=1, source_target_pairs={{0,3},{1,0},{2,1},{3,2},{4,7},{5,4},{6,5},{7,6},{8,11},{9,8},{10,9... | collective-permute-start | bytes 98312 | tf_op jit(solution)/shard_map/ppermute | solution.py:29
  221.7 4.8 %collective-permute-start.15 = (f32[2,32,128]{2,1,0:T(8,128)S(1)}, f32[2,32,128]{2,1,0:T(8,128)S(1)}, u32[]{:S(2)}, u32[]{:S(2)}) collective-permute-start(f32[2,32,128]{2,1,0:T(8,128)S(1)} %get-tuple-element.54), channel_id=1, source_target_pairs={{0,2},{1,3},{2,0},{3,1},{4,6},{5,7},{6,4},{7,5},{8,10},{9,11},{10,... | collective-permute-start | bytes 98312 | tf_op jit(solution)/shard_map/ppermute | solution.py:29
where the time goes:
time: 231 us; the launch traced here: 228 us
  Pallas kernels  98.2 us (43%)
  waiting for transfers between devices  71.3 us (31%)
  local copies, waits for them, and re-layouts  21.5 us (9%)
  starting transfers between devices  17.7 us (8%)
  other arithmetic  17.5 us (8%)
    pallas_call x16, Pallas kernels, kernel_step(): pl.pallas_call(_step_kernel, out_shape=jax.ShapeDtypeStruct(adj.shape, ad...  98.2 us
    ppermute x12, waiting for transfers between devices, swap_over(): lax.ppermute(value, 'space', [(i, i ^ partner_bit) for i in range(count)])  42.9 us
    ppermute x4, waiting for transfers between devices, passed_along(): return lax.ppermute(value, axis, pairs)  25.5 us
    ppermute x4, starting transfers between devices, passed_along(): return lax.ppermute(value, axis, pairs)  8.98 us
    ppermute x12, starting transfers between devices, swap_over(): lax.ppermute(value, 'space', [(i, i ^ partner_bit) for i in range(count)])  8.76 us
    slice x12, local copies, waits for them, and re-layouts, sensitivity(): a_loc = own_cells(adj[:3], 1)  8.48 us
    squeeze x4, local copies, waits for them, and re-layouts, whole_grid_body(): inputs_all[top - chunk + j] = piece[j]  6.29 us
  transfers between devices with their start and end apart: 17, of which 6 were waited for; matrix products, arithmetic and copies ran while one was open for 4% of the time, Pallas kernels for 0%

commit v1 on v0

--- a/solution.py
+++ b/solution.py
@@ -198,66 +198,89 @@
     return in_space_order(me, axis, local, near, far, relay)
 
 
-def _shifted(f, axis, edge):
-    n = f.shape[axis]
-    idx = lax.broadcasted_iota(jnp.int32, f.shape, axis)
-    up = pltpu.roll(f, n - 1, axis)
-    down = pltpu.roll(f, 1, axis)
-    up = jnp.where(idx == n - 1, f if edge else 0.0, up)
-    down = jnp.where(idx == 0, f if edge else 0.0, down)
+def _lane_pair(f, edge):
+    n = f.shape[1]
+    lane = lax.broadcasted_iota(jnp.int32, f.shape, 1)
+    up = jnp.where(lane == n - 1, f if edge else 0.0, pltpu.roll(f, n - 1, 1))
+    down = jnp.where(lane == 0, f if edge else 0.0, pltpu.roll(f, 1, 1))
     return up, down
 
 
-def _step_kernel(adj_ref, inp_ref, alpha_ref, solid_ref, ent_ref, out_ref):
+def _row_pair(f, before, after, first, last, edge):
+    n = f.shape[0]
+    row = lax.broadcasted_iota(jnp.int32, f.shape, 0)
+    up = jnp.where(row == n - 1, pltpu.roll(after, n - 1, 0), pltpu.roll(f, n - 1, 0))
+    down = jnp.where(row == 0, pltpu.roll(before, 1, 0), pltpu.roll(f, 1, 0))
+    up = jnp.where(last & (row == n - 1), f if edge else 0.0, up)
+    down = jnp.where(first & (row == 0), f if edge else 0.0, down)
+    return up, down
+
+
+STRIP = 16
+
+
+def _strip_kernel(adj_ref, inp_ref, alpha_ref, solid_ref, ent_ref, out_ref):
     cells = adj_ref.shape[1]
-    floor = ent_ref[...]
-    for i in range(cells):
-        lo = max(i - 1, 0)
-        hi = min(i + 1, cells - 1)
-        u = [inp_ref[d, i].astype(jnp.float32) for d in range(3)]
-        t = inp_ref[3, i].astype(jnp.float32)
-        t_hi = inp_ref[3, hi].astype(jnp.float32)
-        t_lo = inp_ref[3, lo].astype(jnp.float32)
-        t_r = _shifted(t, 0, True)
-        t_l = _shifted(t, 1, True)
+    strips = adj_ref.shape[2] // STRIP
+
+    def body(n, carry):
+        i = n // strips
+        k = n % strips
+        hi = jnp.minimum(i + 1, cells - 1)
+        lo = jnp.maximum(i - 1, 0)
+        rows = pl.ds(pl.multiple_of(k * STRIP, STRIP), STRIP)
+        before = pl.ds(pl.multiple_of(jnp.maximum(k - 1, 0) * STRIP, STRIP), STRIP)
+        after = pl.ds(pl.multiple_of(jnp.minimum(k + 1, strips - 1) * STRIP, STRIP), STRIP)
+        first = k == 0
+        last = k == strips - 1
+        top_plane = i == cells - 1
+        bottom_plane = i == 0
+
+        def field(ref, c, cast):
+            g = lambda p, r: ref[c, p, r, :].astype(jnp.float32) if cast else ref[c, p, r, :]
+            return g(i, rows), g(hi, rows), g(lo, rows), g(i, before), g(i, after)
+
+        u = [inp_ref[d, i, rows, :].astype(jnp.float32) for d in range(3)]
+        t, t_hi, t_lo, t_b, t_a = field(inp_ref, 3, True)
+        t_r = _row_pair(t, t_b, t_a, first, last, True)
+        t_l = _lane_pair(t, True)
         grad_t = (0.5 * (t_hi - t_lo), 0.5 * (t_r[0] - t_r[1]), 0.5 * (t_l[0] - t_l[1]))
-        b = adj_ref[3, i]
-        b_hi = adj_ref[3, hi]
-        if i == 0:
-            b_lo = jnp.where(floor == 1.0, 0.0, b)
-        else:
-            b_lo = adj_ref[3, lo]
-        alpha = alpha_ref[i]
-        solid = solid_ref[i]
+        b, b_hi, b_lo, b_b, b_a = field(adj_ref, 3, False)
+        b_lo = jnp.where(bottom_plane & (ent_ref[rows, :] == 1.0), 0.0, b_lo)
+        alpha = alpha_ref[i, rows, :]
+        solid = solid_ref[i, rows, :]
         for c in range(3):
-            a = adj_ref[c, i]
-            a_hi = adj_ref[c, hi] if i + 1 < cells else jnp.zeros_like(a)
-            a_lo = adj_ref[c, lo] if i > 0 else jnp.zeros_like(a)
-            a_r = _shifted(a, 0, False)
-            a_l = _shifted(a, 1, False)
+            a, a_hi, a_lo, a_b, a_a = field(adj_ref, c, False)
+            a_hi = jnp.where(top_plane, 0.0, a_hi)
+            a_lo = jnp.where(bottom_plane, 0.0, a_lo)
+            a_r = _row_pair(a, a_b, a_a, first, last, False)
+            a_l = _lane_pair(a, False)
             lap = (a_hi + a_lo) + a_r[0] + a_r[1] + a_l[0] + a_l[1] - 6.0 * a
-            carry = (
+            carry_a = (
                 u[0] * (0.5 * (a_hi - a_lo))
                 + u[1] * (0.5 * (a_r[0] - a_r[1]))
                 + u[2] * (0.5 * (a_l[0] - a_l[1]))
             )
-            out_ref[c, i] = a + 0.1 * (1.2 * lap + carry - alpha * a - b * grad_t[c])
-        b_r = _shifted(b, 0, True)
-        b_l = _shifted(b, 1, True)
+            out_ref[c, i, rows, :] = a + 0.1 * (1.2 * lap + carry_a - alpha * a - b * grad_t[c])
+        b_r = _row_pair(b, b_b, b_a, first, last, True)
+        b_l = _lane_pair(b, True)
         lap_b = (b_hi + b_lo) + b_r[0] + b_r[1] + b_l[0] + b_l[1] - 6.0 * b
         carry_b = (
             u[0] * (0.5 * (b_hi - b_lo))
             + u[1] * (0.5 * (b_r[0] - b_r[1]))
             + u[2] * (0.5 * (b_l[0] - b_l[1]))
         )
-        out_ref[3, i] = b + 0.1 * (1.2 * lap_b + carry_b - 2.0 * solid * b + 2.0 * solid)
+        out_ref[3, i, rows, :] = b + 0.1 * (1.2 * lap_b + carry_b - 2.0 * solid * b + 2.0 * solid)
+        return carry
+
+    lax.fori_loop(0, cells * strips, body, 0)
 
 
 def kernel_step(adj, inputs, alpha, solid, floor):
     vmem = pl.BlockSpec(memory_space=pltpu.VMEM)
     n = adj.size
     return pl.pallas_call(
-        _step_kernel,
+        _strip_kernel,
         out_shape=jax.ShapeDtypeStruct(adj.shape, adj.dtype),
         in_specs=[vmem] * 5,
         out_specs=vmem,

time: 231 us -> 286 us (1.24)
  Pallas kernels: 98.2 us -> 157 us
    pallas_call x16, Pallas kernels: 98.2 us -> 157 us  [kernel_step(): pl.pallas_call(_strip_kernel, out_shape=jax.ShapeDtypeStruct(adj.shape, a...]
  transfers between devices with their start and end apart: 17 -> 17, of which waited for: 6 -> 6; matrix products, arithmetic and copies ran while one was open for 4% -> 3% of each run, Pallas kernels for 0% -> 0%
where the time goes in v1:
time: 286 us; the launch traced here: 285 us
  Pallas kernels  157 us (55%)
  waiting for transfers between devices  71.3 us (25%)
  local copies, waits for them, and re-layouts  21.5 us (8%)
  starting transfers between devices  17.5 us (6%)
  other arithmetic  17 us (6%)
    pallas_call x16, Pallas kernels, kernel_step(): pl.pallas_call(_strip_kernel, out_shape=jax.ShapeDtypeStruct(adj.shape, a...  157 us
    ppermute x12, waiting for transfers between devices, swap_over(): lax.ppermute(value, 'space', [(i, i ^ partner_bit) for i in range(count)])  42.9 us
    ppermute x4, waiting for transfers between devices, passed_along(): return lax.ppermute(value, axis, pairs)  25.5 us
    ppermute x4, starting transfers between devices, passed_along(): return lax.ppermute(value, axis, pairs)  8.77 us
    ppermute x12, starting transfers between devices, swap_over(): lax.ppermute(value, 'space', [(i, i ^ partner_bit) for i in range(count)])  8.76 us
    slice x12, local copies, waits for them, and re-layouts, sensitivity(): a_loc = own_cells(adj[:3], 1)  8.48 us
    squeeze x4, local copies, waits for them, and re-layouts, whole_grid_body(): inputs_all[top - chunk + j] = piece[j]  6.29 us
  transfers between devices with their start and end apart: 17, of which 6 were waited for; matrix products, arithmetic and copies ran while one was open for 3% of the time, Pallas kernels for 0%

profile of v1, /device:TPU:0, one launch (start us, length us, event | category | flops | bytes accessed | tf_op | source)
XLA Modules:
  0.0 285.2 jit_solution(4818639882933251480)
XLA Ops:
  0.7 3.2 %pad_maximum_fusion = bf16[8,4,2,128,128]{4,3,2,1,0:T(8,128)(2,1)} fusion(bf16[8,1,2,128,128]{4,3,2,1,0:T(8,128)(2,1)} %bitcast.102, bf16[8,3,2,128,128]{4,3,2,1,0:T(8,128)(2,1)} %param.5), kind=kLoop, calls=%fused_computation.4 | loop fusion | flops 1048576 | bytes 4194304 | tf_op jit(solution)/shard_map/concatenate | solution.py:302
  3.9 0.5 collective-permute-start.2
  4.4 0.2 fusion.3
  4.6 2.6 collective-permute-start.10
  7.2 0.1 collective-permute-start.6
  7.3 2.0 collective-permute-start.3
  9.3 24.5 %collective-permute-done.3 = f32[2,128,128]{2,1,0:T(8,128)S(1)} collective-permute-done((f32[2,128,128]{2,1,0:T(8,128)S(1)}, f32[2,128,128]{2,1,0:T(8,128)S(1)}, u32[]{:S(2)}, u32[]{:S(2)}) %collective-permute-start.3) | collective-permute-done | bytes 131104 | tf_op jit(solution)/shard_map/ppermute | solution.py:172
  33.8 1.8 collective-permute-start.8
  35.7 1.3 collective-permute-start
  37.0 0.5 collective-permute-start.7
  37.4 1.5 convert_element_type.87.ent_ref
  38.9 1.1 broadcast_select_fusion.39
  40.0 1.1 fusion.12
  41.1 7.7 %collective-permute-done.8 = bf16[2,4,2,128,128]{4,3,2,1,0:T(8,128)(2,1)} collective-permute-done((bf16[2,4,2,128,128]{4,3,2,1,0:T(8,128)(2,1)S(1)}, bf16[2,4,2,128,128]{4,3,2,1,0:T(8,128)(2,1)}, u32[]{:S(2)}, u32[]{:S(2)}) %collective-permute-start.8) | collective-permute-done | bytes 524320 | tf_op jit(solution)/shard_map/ppermute | solution.py:172
  48.8 10.7 %collective-permute-done = bf16[2,4,2,128,128]{4,3,2,1,0:T(8,128)(2,1)} collective-permute-done((bf16[2,4,2,128,128]{4,3,2,1,0:T(8,128)(2,1)S(1)}, bf16[2,4,2,128,128]{4,3,2,1,0:T(8,128)(2,1)}, u32[]{:S(2)}, u32[]{:S(2)}) %collective-permute-start) | collective-permute-done | bytes 524320 | tf_op jit(solution)/shard_map/ppermute | solution.py:172
  59.6 1.9 broadcast_select_fusion.19
  61.4 0.6 pad_maximum_fusion.2
  62.0 1.6 slice_bitcast_fusion.4
  63.6 1.6 broadcast_select_fusion.23
  65.2 0.6 pad_maximum_fusion.1
  65.8 1.6 slice_bitcast_fusion.6
  67.4 1.6 slice_bitcast_fusion.2
  68.9 1.6 slice_bitcast_fusion
  70.5 1.6 broadcast_in_dim.14.adj_ref
  72.1 9.8 %shard_map.68.adj_ref = f32[4,8,128,128]{3,2,1,0:T(8,128)} custom-call(f32[4,8,128,128]{3,2,1,0:T(8,128)} %broadcast_in_dim.14.adj_ref, bf16[4,8,128,128]{3,2,1,0:T(8,128)(2,1)} %get-tuple-element.45.inp_ref, f32[8,128,128]{2,1,0:T(8,128)} %get-tuple-element.47.alpha_ref, f32[8,128,128]{2,1,0:T(8,128)} %get-tuple-element.46.solid_ref, ...), custom_call_target="tpu_custom_call" | custom-call | flops 20971520 | bytes 6291456 | tf_op jit(solution)/shard_map/pallas_call | solution.py:282
  81.9 9.8 %shard_map.69.adj_ref = f32[4,8,128,128]{3,2,1,0:T(8,128)} custom-call(f32[4,8,128,128]{3,2,1,0:T(8,128)} %shard_map.68.adj_ref, bf16[4,8,128,128]{3,2,1,0:T(8,128)(2,1)} %get-tuple-element.44.inp_ref, f32[8,128,128]{2,1,0:T(8,128)} %get-tuple-element.47.alpha_ref, f32[8,128,128]{2,1,0:T(8,128)} %get-tuple-element.46.solid_ref, ...), custom_call_target="tpu_custom_call" | custom-call | flops 20971520 | bytes 6291456 | tf_op jit(solution)/shard_map/pallas_call | solution.py:282
  91.6 9.8 %shard_map.70.adj_ref = f32[4,8,128,128]{3,2,1,0:T(8,128)} custom-call(f32[4,8,128,128]{3,2,1,0:T(8,128)} %shard_map.69.adj_ref, bf16[4,8,128,128]{3,2,1,0:T(8,128)(2,1)} %get-tuple-element.43.inp_ref, f32[8,128,128]{2,1,0:T(8,128)} %get-tuple-element.47.alpha_ref, f32[8,128,128]{2,1,0:T(8,128)} %get-tuple-element.46.solid_ref, ...), custom_call_target="tpu_custom_call" | custom-call | flops 20971520 | bytes 6291456 | tf_op jit(solution)/shard_map/pallas_call | solution.py:282
  101.4 9.8 %shard_map.71.adj_ref = f32[4,8,128,128]{3,2,1,0:T(8,128)} custom-call(f32[4,8,128,128]{3,2,1,0:T(8,128)} %shard_map.70.adj_ref, bf16[4,8,128,128]{3,2,1,0:T(8,128)(2,1)} %get-tuple-element.42.inp_ref, f32[8,128,128]{2,1,0:T(8,128)} %get-tuple-element.47.alpha_ref, f32[8,128,128]{2,1,0:T(8,128)} %get-tuple-element.46.solid_ref, ...), custom_call_target="tpu_custom_call" | custom-call | flops 20971520 | bytes 6291456 | tf_op jit(solution)/shard_map/pallas_call | solution.py:282
  111.2 9.8 %shard_map.72.adj_ref = f32[4,8,128,128]{3,2,1,0:T(8,128)} custom-call(f32[4,8,128,128]{3,2,1,0:T(8,128)} %shard_map.71.adj_ref, bf16[4,8,128,128]{3,2,1,0:T(8,128)(2,1)} %get-tuple-element.37.inp_ref, f32[8,128,128]{2,1,0:T(8,128)} %get-tuple-element.47.alpha_ref, f32[8,128,128]{2,1,0:T(8,128)} %get-tuple-element.46.solid_ref, ...), custom_call_target="tpu_custom_call" | custom-call | flops 20971520 | bytes 6291456 | tf_op jit(solution)/shard_map/pallas_call | solution.py:282
  120.9 9.8 %shard_map.73.adj_ref = f32[4,8,128,128]{3,2,1,0:T(8,128)} custom-call(f32[4,8,128,128]{3,2,1,0:T(8,128)} %shard_map.72.adj_ref, bf16[4,8,128,128]{3,2,1,0:T(8,128)(2,1)} %get-tuple-element.36.inp_ref, f32[8,128,128]{2,1,0:T(8,128)} %get-tuple-element.47.alpha_ref, f32[8,128,128]{2,1,0:T(8,128)} %get-tuple-element.46.solid_ref, ...), custom_call_target="tpu_custom_call" | custom-call | flops 20971520 | bytes 6291456 | tf_op jit(solution)/shard_map/pallas_call | solution.py:282
  130.7 9.8 %shard_map.74.adj_ref = f32[4,8,128,128]{3,2,1,0:T(8,128)} custom-call(f32[4,8,128,128]{3,2,1,0:T(8,128)} %shard_map.73.adj_ref, bf16[4,8,128,128]{3,2,1,0:T(8,128)(2,1)} %get-tuple-element.27.inp_ref, f32[8,128,128]{2,1,0:T(8,128)} %get-tuple-element.47.alpha_ref, f32[8,128,128]{2,1,0:T(8,128)} %get-tuple-element.46.solid_ref, ...), custom_call_target="tpu_custom_call" | custom-call | flops 20971520 | bytes 6291456 | tf_op jit(solution)/shard_map/pallas_call | solution.py:282
  140.5 9.8 %shard_map.75 = f32[4,8,128,128]{3,2,1,0:T(8,128)} custom-call(f32[4,8,128,128]{3,2,1,0:T(8,128)} %shard_map.74.adj_ref, bf16[4,8,128,128]{3,2,1,0:T(8,128)(2,1)} %get-tuple-element.26.inp_ref, f32[8,128,128]{2,1,0:T(8,128)} %get-tuple-element.47.alpha_ref, f32[8,128,128]{2,1,0:T(8,128)} %get-tuple-element.46.solid_ref, f32[128,128]{1,0:T(8,128)} %convert_element_type.87.ent_ref), custom_call_target="tpu_custom_call" | custom-call | flops 20971520 | bytes 6291456 | tf_op jit(solution)/shard_map/pallas_call | solution.py:282
  150.3 1.3 constant_dynamic-slice_fusion
  151.6 3.9 %collective-permute-start.12 = (f32[2,8,128,128]{3,2,1,0:T(8,128)S(1)}, f32[2,8,128,128]{3,2,1,0:T(8,128)S(1)}, u32[]{:S(2)}, u32[]{:S(2)}) collective-permute-start(f32[2,8,128,128]{3,2,1,0:T(8,128)S(1)} %constant_dynamic-slice_fusion), channel_id=1, source_target_pairs={{0,3},{1,0},{2,1},{3,2},{4,7},{5,4},{6,5},{7,6},{8,11},{9,8},{10,9... | collective-permute-start | bytes 3145736 | tf_op jit(solution)/shard_map/ppermute | solution.py:29
  155.5 23.1 %collective-permute-done.12 = f32[2,8,128,128]{3,2,1,0:T(8,128)S(1)} collective-permute-done((f32[2,8,128,128]{3,2,1,0:T(8,128)S(1)}, f32[2,8,128,128]{3,2,1,0:T(8,128)S(1)}, u32[]{:S(2)}, u32[]{:S(2)}) %collective-permute-start.12) | collective-permute-done | bytes 1048608 | tf_op jit(solution)/shard_map/ppermute | solution.py:29
  178.5 2.8 collective-permute-done.13
  181.3 1.8 maximum_select_fusion.adj_ref
  183.1 1.3 copy-done.3
  184.4 9.8 %shard_map.76.adj_ref = f32[4,8,128,128]{3,2,1,0:T(8,128)} custom-call(f32[4,8,128,128]{3,2,1,0:T(8,128)} %copy-done.3, bf16[4,8,128,128]{3,2,1,0:T(8,128)(2,1)} %get-tuple-element.45.inp_ref, f32[8,128,128]{2,1,0:T(8,128)} %get-tuple-element.47.alpha_ref, f32[8,128,128]{2,1,0:T(8,128)} %get-tuple-element.46.solid_ref, f32[128,128]{1,0:T(8,128)} %convert_element_type.87.ent_ref), custom_call_target="tpu_custom_call" | custom-call | flops 20971520 | bytes 6291456 | tf_op jit(solution)/shard_map/pallas_call | solution.py:282
  194.2 2.7 slice.212
  196.9 9.8 %shard_map.77.adj_ref = f32[4,8,128,128]{3,2,1,0:T(8,128)} custom-call(f32[4,8,128,128]{3,2,1,0:T(8,128)} %shard_map.76.adj_ref, bf16[4,8,128,128]{3,2,1,0:T(8,128)(2,1)} %get-tuple-element.44.inp_ref, f32[8,128,128]{2,1,0:T(8,128)} %get-tuple-element.47.alpha_ref, f32[8,128,128]{2,1,0:T(8,128)} %get-tuple-element.46.solid_ref, ...), custom_call_target="tpu_custom_call" | custom-call | flops 20971520 | bytes 6291456 | tf_op jit(solution)/shard_map/pallas_call | solution.py:282
  206.7 9.8 %shard_map.78.adj_ref = f32[4,8,128,128]{3,2,1,0:T(8,128)} custom-call(f32[4,8,128,128]{3,2,1,0:T(8,128)} %shard_map.77.adj_ref, bf16[4,8,128,128]{3,2,1,0:T(8,128)(2,1)} %get-tuple-element.43.inp_ref, f32[8,128,128]{2,1,0:T(8,128)} %get-tuple-element.47.alpha_ref, f32[8,128,128]{2,1,0:T(8,128)} %get-tuple-element.46.solid_ref, ...), custom_call_target="tpu_custom_call" | custom-call | flops 20971520 | bytes 6291456 | tf_op jit(solution)/shard_map/pallas_call | solution.py:282
  216.6 9.8 %shard_map.79.adj_ref = f32[4,8,128,128]{3,2,1,0:T(8,128)} custom-call(f32[4,8,128,128]{3,2,1,0:T(8,128)} %shard_map.78.adj_ref, bf16[4,8,128,128]{3,2,1,0:T(8,128)(2,1)} %get-tuple-element.42.inp_ref, f32[8,128,128]{2,1,0:T(8,128)} %get-tuple-element.47.alpha_ref, f32[8,128,128]{2,1,0:T(8,128)} %get-tuple-element.46.solid_ref, ...), custom_call_target="tpu_custom_call" | custom-call | flops 20971520 | bytes 6291456 | tf_op jit(solution)/shard_map/pallas_call | solution.py:282
  226.3 10.0 %shard_map.80.adj_ref = f32[4,8,128,128]{3,2,1,0:T(8,128)} custom-call(f32[4,8,128,128]{3,2,1,0:T(8,128)} %shard_map.79.adj_ref, bf16[4,8,128,128]{3,2,1,0:T(8,128)(2,1)} %get-tuple-element.37.inp_ref, f32[8,128,128]{2,1,0:T(8,128)} %get-tuple-element.47.alpha_ref, f32[8,128,128]{2,1,0:T(8,128)} %get-tuple-element.46.solid_ref, ...), custom_call_target="tpu_custom_call" | custom-call | flops 20971520 | bytes 6291456 | tf_op jit(solution)/shard_map/pallas_call | solution.py:282
  236.3 1.3 slice.220
  237.6 9.9 %shard_map.81.adj_ref = f32[4,8,128,128]{3,2,1,0:T(8,128)} custom-call(f32[4,8,128,128]{3,2,1,0:T(8,128)} %shard_map.80.adj_ref, bf16[4,8,128,128]{3,2,1,0:T(8,128)(2,1)} %get-tuple-element.36.inp_ref, f32[8,128,128]{2,1,0:T(8,128)} %get-tuple-element.47.alpha_ref, f32[8,128,128]{2,1,0:T(8,128)} %get-tuple-element.46.solid_ref, ...), custom_call_target="tpu_custom_call" | custom-call | flops 20971520 | bytes 6291456 | tf_op jit(solution)/shard_map/pallas_call | solution.py:282
  247.5 1.3 slice.222
  248.7 9.9 %shard_map.82.adj_ref = f32[4,8,128,128]{3,2,1,0:T(8,128)} custom-call(f32[4,8,128,128]{3,2,1,0:T(8,128)} %shard_map.81.adj_ref, bf16[4,8,128,128]{3,2,1,0:T(8,128)(2,1)} %get-tuple-element.27.inp_ref, f32[8,128,128]{2,1,0:T(8,128)} %get-tuple-element.47.alpha_ref, f32[8,128,128]{2,1,0:T(8,128)} %get-tuple-element.46.solid_ref, ...), custom_call_target="tpu_custom_call" | custom-call | flops 20971520 | bytes 6291456 | tf_op jit(solution)/shard_map/pallas_call | solution.py:282
  258.7 1.3 slice.224
  260.0 9.9 %shard_map.83 = f32[4,8,128,128]{3,2,1,0:T(8,128)} custom-call(f32[4,8,128,128]{3,2,1,0:T(8,128)} %shard_map.82.adj_ref, bf16[4,8,128,128]{3,2,1,0:T(8,128)(2,1)} %get-tuple-element.26.inp_ref, f32[8,128,128]{2,1,0:T(8,128)} %get-tuple-element.47.alpha_ref, f32[8,128,128]{2,1,0:T(8,128)} %get-tuple-element.46.solid_ref, f32[128,128]{1,0:T(8,128)} %convert_element_type.87.ent_ref), custom_call_target="tpu_custom_call" | custom-call | flops 20971520 | bytes 6291456 | tf_op jit(solution)/shard_map/pallas_call | solution.py:282
  269.9 1.4 slice-done.1
  271.3 0.5 slice-done.3
  271.8 2.7 fusion.11
  274.5 0.0 slice-done.9
  274.6 0.2 slice-done.10
  274.7 0.2 slice-done.11
  274.9 0.2 copy-done.6
  275.1 0.3 fusion.14
  275.4 0.5 collective-permute-start.14
  275.9 3.9 %collective-permute-start.16 = (f32[2,32,128]{2,1,0:T(8,128)S(1)}, f32[2,32,128]{2,1,0:T(8,128)S(1)}, u32[]{:S(2)}, u32[]{:S(2)}) collective-permute-start(f32[2,32,128]{2,1,0:T(8,128)S(1)} %get-tuple-element.53), channel_id=1, source_target_pairs={{0,3},{1,0},{2,1},{3,2},{4,7},{5,4},{6,5},{7,6},{8,11},{9,8},{10,9... | collective-permute-start | bytes 98312 | tf_op jit(solution)/shard_map/ppermute | solution.py:29
  279.8 0.5 collective-permute-start.15
  280.3 1.9 dynamic-slice_bitcast_fusion
  282.1 2.4 collective-permute-done.15
  284.6 0.6 fusion.22
  (66 shorter events, 0.2 us)
Async XLA Ops:
  0.6 3.8 %copy-start.4 = (bf16[8,3,2,128,128]{4,3,2,1,0:T(8,128)(2,1)S(1)}, bf16[8,3,2,128,128]{4,3,2,1,0:T(8,128)(2,1)}, u32[]{:S(2)}) copy-start(bf16[8,3,2,128,128]{4,3,2,1,0:T(8,128)(2,1)} %param.5) | copy-start | bytes 4718596
  0.6 3.8 %copy-start.5 = (bf16[8,2,128,128]{3,2,1,0:T(8,128)(2,1)S(1)}, bf16[8,2,128,128]{3,2,1,0:T(8,128)(2,1)}, u32[]{:S(2)}) copy-start(bf16[8,2,128,128]{3,2,1,0:T(8,128)(2,1)} %param.6) | copy-start | bytes 1572868
  3.9 3.4 %copy-start.11 = (s32[2,128,128]{2,1,0:T(8,128)S(1)}, s32[2,128,128]{2,1,0:T(8,128)}, u32[]{:S(2)}) copy-start(s32[2,128,128]{2,1,0:T(8,128)} %param.8) | copy-start | bytes 393220
  3.9 3.4 %copy-start.12 = (f32[2,128,128]{2,1,0:T(8,128)S(1)}, f32[2,128,128]{2,1,0:T(8,128)}, u32[]{:S(2)}) copy-start(f32[2,128,128]{2,1,0:T(8,128)} %param.7) | copy-start | bytes 393220
  3.9 55.6 %collective-permute-start.2 = (bf16[8,4,2,128,128]{4,3,2,1,0:T(8,128)(2,1)}, bf16[8,4,2,128,128]{4,3,2,1,0:T(8,128)(2,1)S(1)}, u32[]{:S(2)}, u32[]{:S(2)}) collective-permute-start(bf16[8,4,2,128,128]{4,3,2,1,0:T(8,128)(2,1)} %pad_maximum_fusion), channel_id=1, source_target_pairs={{0,4},{4,0},{8,12},{12,8},{1,5},{5,1},{9,13},{13,9},{2,6},{6,2},{1... | collective-permute-start | bytes 6291464 | tf_op jit(solution)/shard_map/ppermute | solution.py:172
  4.6 31.1 %copy-start.7 = (bf16[2,4,2,128,128]{4,3,2,1,0:T(8,128)(2,1)}, bf16[2,4,2,128,128]{4,3,2,1,0:T(8,128)(2,1)S(1)}, u32[]{:S(2)}) copy-start(bf16[2,4,2,128,128]{4,3,2,1,0:T(8,128)(2,1)S(1)} %get-tuple-element.32) | copy-start | bytes 1572868
  4.6 32.3 %copy-start.9 = (bf16[2,4,2,128,128]{4,3,2,1,0:T(8,128)(2,1)}, bf16[2,4,2,128,128]{4,3,2,1,0:T(8,128)(2,1)S(1)}, u32[]{:S(2)}) copy-start(bf16[2,4,2,128,128]{4,3,2,1,0:T(8,128)(2,1)S(1)} %get-tuple-element.34) | copy-start | bytes 1572868
  4.6 32.3 %collective-permute-start.10 = (bf16[2,4,2,128,128]{4,3,2,1,0:T(8,128)(2,1)S(1)}, bf16[2,4,2,128,128]{4,3,2,1,0:T(8,128)(2,1)}, u32[]{:S(2)}, u32[]{:S(2)}) collective-permute-start(bf16[2,4,2,128,128]{4,3,2,1,0:T(8,128)(2,1)S(1)} %get-tuple-element.32), channel_id=1, source_target_pairs={{0,8},{4,12},{8,0},{12,4},{1,9},{5,13},{9,1},{13,5},{2,10},{6,14},... | collective-permute-start | bytes 1572872 | tf_op jit(solution)/shard_map/ppermute | solution.py:172
  7.2 29.7 %collective-permute-start.6 = (bf16[2,4,2,128,128]{4,3,2,1,0:T(8,128)(2,1)S(1)}, bf16[2,4,2,128,128]{4,3,2,1,0:T(8,128)(2,1)}, u32[]{:S(2)}, u32[]{:S(2)}) collective-permute-start(bf16[2,4,2,128,128]{4,3,2,1,0:T(8,128)(2,1)S(1)} %get-tuple-element.34), channel_id=1, source_target_pairs={{0,8},{4,12},{8,0},{12,4},{1,9},{5,13},{9,1},{13,5},{2,10},{6,14},... | collective-permute-start | bytes 1572872 | tf_op jit(solution)/shard_map/ppermute | solution.py:172
  7.3 26.5 %collective-permute-start.3 = (f32[2,128,128]{2,1,0:T(8,128)S(1)}, f32[2,128,128]{2,1,0:T(8,128)S(1)}, u32[]{:S(2)}, u32[]{:S(2)}) collective-permute-start(f32[2,128,128]{2,1,0:T(8,128)S(1)} %compare_select_fusion), channel_id=1, source_target_pairs={{0,8},{4,12},{8,0},{12,4},{1,9},{5,13},{9,1},{13,5},{2,10},{6,14},... | collective-permute-start | bytes 393224 | tf_op jit(solution)/shard_map/ppermute | solution.py:172
  9.3 24.5 %collective-permute-start.5 = (f32[2,128,128]{2,1,0:T(8,128)S(1)}, f32[2,128,128]{2,1,0:T(8,128)S(1)}, u32[]{:S(2)}, u32[]{:S(2)}) collective-permute-start(f32[2,128,128]{2,1,0:T(8,128)S(1)} %compare_select_fusion), channel_id=1, source_target_pairs={{0,4},{4,0},{8,12},{12,8},{1,5},{5,1},{9,13},{13,9},{2,6},{6,2},{1... | collective-permute-start | bytes 393224 | tf_op jit(solution)/shard_map/ppermute | solution.py:172
  33.8 1.8 collective-permute-start.4
  33.8 3.1 %copy-start.13 = (f32[2,128,128]{2,1,0:T(8,128)}, f32[2,128,128]{2,1,0:T(8,128)S(1)}, u32[]{:S(2)}) copy-start(f32[2,128,128]{2,1,0:T(8,128)S(1)} %collective-permute-done.5) | copy-start | bytes 393220
  33.8 15.0 %collective-permute-start.8 = (bf16[2,4,2,128,128]{4,3,2,1,0:T(8,128)(2,1)S(1)}, bf16[2,4,2,128,128]{4,3,2,1,0:T(8,128)(2,1)}, u32[]{:S(2)}, u32[]{:S(2)}) collective-permute-start(bf16[2,4,2,128,128]{4,3,2,1,0:T(8,128)(2,1)S(1)} %get-tuple-element.33), channel_id=1, source_target_pairs={{0,8},{4,12},{8,0},{12,4},{1,9},{5,13},{9,1},{13,5},{2,10},{6,14},... | collective-permute-start | bytes 1572872 | tf_op jit(solution)/shard_map/ppermute | solution.py:172
  35.6 1.8 copy-start.14
  35.7 23.9 %collective-permute-start = (bf16[2,4,2,128,128]{4,3,2,1,0:T(8,128)(2,1)S(1)}, bf16[2,4,2,128,128]{4,3,2,1,0:T(8,128)(2,1)}, u32[]{:S(2)}, u32[]{:S(2)}) collective-permute-start(bf16[2,4,2,128,128]{4,3,2,1,0:T(8,128)(2,1)S(1)} %get-tuple-element.35), channel_id=1, source_target_pairs={{0,8},{4,12},{8,0},{12,4},{1,9},{5,13},{9,1},{13,5},{2,10},{6,14},... | collective-permute-start | bytes 1572872 | tf_op jit(solution)/shard_map/ppermute | solution.py:172
  36.9 22.6 %collective-permute-start.11 = (bf16[2,4,2,128,128]{4,3,2,1,0:T(8,128)(2,1)}, bf16[2,4,2,128,128]{4,3,2,1,0:T(8,128)(2,1)}, u32[]{:S(2)}, u32[]{:S(2)}) collective-permute-start(bf16[2,4,2,128,128]{4,3,2,1,0:T(8,128)(2,1)} %collective-permute-done.10), channel_id=1, source_target_pairs={{0,4},{4,0},{8,12},{12,8},{1,5},{5,1},{9,13},{13,9},{2,6},{6,2},{1... | collective-permute-start | bytes 1572872 | tf_op jit(solution)/shard_map/ppermute | solution.py:172
  37.0 22.6 %collective-permute-start.7 = (bf16[2,4,2,128,128]{4,3,2,1,0:T(8,128)(2,1)}, bf16[2,4,2,128,128]{4,3,2,1,0:T(8,128)(2,1)}, u32[]{:S(2)}, u32[]{:S(2)}) collective-permute-start(bf16[2,4,2,128,128]{4,3,2,1,0:T(8,128)(2,1)} %collective-permute-done.6), channel_id=1, source_target_pairs={{0,4},{4,0},{8,12},{12,8},{1,5},{5,1},{9,13},{13,9},{2,6},{6,2},{1... | collective-permute-start | bytes 1572872 | tf_op jit(solution)/shard_map/ppermute | solution.py:172
  38.9 20.6 %copy-start.8 = (bf16[2,4,2,128,128]{4,3,2,1,0:T(8,128)(2,1)S(1)}, bf16[2,4,2,128,128]{4,3,2,1,0:T(8,128)(2,1)}, u32[]{:S(2)}) copy-start(bf16[2,4,2,128,128]{4,3,2,1,0:T(8,128)(2,1)} %copy-done.7) | copy-start | bytes 1572868
  38.9 20.6 %copy-start.10 = (bf16[2,4,2,128,128]{4,3,2,1,0:T(8,128)(2,1)S(1)}, bf16[2,4,2,128,128]{4,3,2,1,0:T(8,128)(2,1)}, u32[]{:S(2)}) copy-start(bf16[2,4,2,128,128]{4,3,2,1,0:T(8,128)(2,1)} %copy-done.9) | copy-start | bytes 1572868
  48.8 14.8 %collective-permute-start.9 = (bf16[2,4,2,128,128]{4,3,2,1,0:T(8,128)(2,1)}, bf16[2,4,2,128,128]{4,3,2,1,0:T(8,128)(2,1)S(1)}, u32[]{:S(2)}, u32[]{:S(2)}) collective-permute-start(bf16[2,4,2,128,128]{4,3,2,1,0:T(8,128)(2,1)} %collective-permute-done.8), channel_id=1, source_target_pairs={{0,4},{4,0},{8,12},{12,8},{1,5},{5,1},{9,13},{13,9},{2,6},{6,2},{1... | collective-permute-start | bytes 1572872 | tf_op jit(solution)/shard_map/ppermute | solution.py:172
  59.5 4.1 %collective-permute-start.1 = (bf16[2,4,2,128,128]{4,3,2,1,0:T(8,128)(2,1)}, bf16[2,4,2,128,128]{4,3,2,1,0:T(8,128)(2,1)S(1)}, u32[]{:S(2)}, u32[]{:S(2)}) collective-permute-start(bf16[2,4,2,128,128]{4,3,2,1,0:T(8,128)(2,1)} %collective-permute-done), channel_id=1, source_target_pairs={{0,4},{4,0},{8,12},{12,8},{1,5},{5,1},{9,13},{13,9},{2,6},{6,2},{1... | collective-permute-start | bytes 1572872 | tf_op jit(solution)/shard_map/ppermute | solution.py:172
  151.6 27.0 %collective-permute-start.12 = (f32[2,8,128,128]{3,2,1,0:T(8,128)S(1)}, f32[2,8,128,128]{3,2,1,0:T(8,128)S(1)}, u32[]{:S(2)}, u32[]{:S(2)}) collective-permute-start(f32[2,8,128,128]{3,2,1,0:T(8,128)S(1)} %constant_dynamic-slice_fusion), channel_id=1, source_target_pairs={{0,3},{1,0},{2,1},{3,2},{4,7},{5,4},{6,5},{7,6},{8,11},{9,8},{10,9... | collective-permute-start | bytes 3145736 | tf_op jit(solution)/shard_map/ppermute | solution.py:29
  178.5 2.8 collective-permute-start.13
  183.1 1.4 copy-start.3
  226.3 10.0 %copy-start = (f32[4,8,128,128]{3,2,1,0:T(8,128)S(1)}, f32[4,8,128,128]{3,2,1,0:T(8,128)}, u32[]{:S(2)}) copy-start(f32[4,8,128,128]{3,2,1,0:T(8,128)} %shard_map.79.adj_ref) | copy-start | bytes 6291460
  237.6 9.9 %copy-start.1 = (f32[4,8,128,128]{3,2,1,0:T(8,128)S(1)}, f32[4,8,128,128]{3,2,1,0:T(8,128)}, u32[]{:S(2)}) copy-start(f32[4,8,128,128]{3,2,1,0:T(8,128)} %shard_map.80.adj_ref) | copy-start | bytes 6291460
  248.7 9.9 %copy-start.2 = (f32[4,8,128,128]{3,2,1,0:T(8,128)S(1)}, f32[4,8,128,128]{3,2,1,0:T(8,128)}, u32[]{:S(2)}) copy-start(f32[4,8,128,128]{3,2,1,0:T(8,128)} %shard_map.81.adj_ref) | copy-start | bytes 6291460
  260.0 9.9 %slice-start.5 = ((f32[4,8,128,128]{3,2,1,0:T(8,128)}), f32[3,8,128,128]{3,2,1,0:T(8,128)S(1)}, s32[]{:S(2)}) async-start(f32[4,8,128,128]{3,2,1,0:T(8,128)} %shard_map.77.adj_ref), calls=%async_computation.5 | async-start | bytes 3145728 | tf_op jit(solution)/shard_map/slice | solution.py:332
  260.0 9.9 %slice-start.7 = ((f32[4,8,128,128]{3,2,1,0:T(8,128)}), f32[3,8,128,128]{3,2,1,0:T(8,128)S(1)}, s32[]{:S(2)}) async-start(f32[4,8,128,128]{3,2,1,0:T(8,128)} %shard_map.78.adj_ref), calls=%async_computation.7 | async-start | bytes 3145728 | tf_op jit(solution)/shard_map/slice | solution.py:332
  269.9 1.4 slice-start.1
  269.9 1.9 slice-start.3
  271.8 2.7 slice-start
  271.8 2.7 slice-start.2
  271.8 2.7 slice-start.4
  271.8 2.8 slice-start.6
  271.8 2.8 slice-start.8
  271.8 2.8 slice-start.9
  271.8 2.9 %slice-start.10 = ((f32[4,8,128,128]{3,2,1,0:T(8,128)}), f32[1,8,128,128]{3,2,1,0:T(8,128)S(1)}, s32[]{:S(2)}) async-start(f32[4,8,128,128]{3,2,1,0:T(8,128)} %shard_map.81.adj_ref), calls=%async_computation.10 | async-start | bytes 1048576 | tf_op jit(solution)/shard_map/slice | solution.py:333
  271.8 3.1 %slice-start.11 = ((f32[4,8,128,128]{3,2,1,0:T(8,128)}), f32[1,8,128,128]{3,2,1,0:T(8,128)S(1)}, s32[]{:S(2)}) async-start(f32[4,8,128,128]{3,2,1,0:T(8,128)} %copy-done.3), calls=%async_computation.11 | async-start | bytes 1048576 | tf_op jit(solution)/shard_map/slice | solution.py:333
  271.8 3.2 %copy-start.6 = (bf16[8,2,128,128]{3,2,1,0:T(8,128)(2,1)S(1)}, bf16[8,2,128,128]{3,2,1,0:T(8,128)(2,1)}, u32[]{:S(2)}) copy-start(bf16[8,2,128,128]{3,2,1,0:T(8,128)(2,1)} %param.6) | copy-start | bytes 1572868
  275.4 6.8 %collective-permute-start.14 = (f32[2,32,128]{2,1,0:T(8,128)S(1)}, f32[2,32,128]{2,1,0:T(8,128)S(1)}, u32[]{:S(2)}, u32[]{:S(2)}) collective-permute-start(f32[2,32,128]{2,1,0:T(8,128)S(1)} %get-tuple-element.52), channel_id=1, source_target_pairs={{0,1},{1,2},{2,3},{3,0},{4,5},{5,6},{6,7},{7,4},{8,9},{9,10},{10,1... | collective-permute-start | bytes 98312 | tf_op jit(solution)/shard_map/ppermute | solution.py:29
  275.9 6.3 %collective-permute-start.16 = (f32[2,32,128]{2,1,0:T(8,128)S(1)}, f32[2,32,128]{2,1,0:T(8,128)S(1)}, u32[]{:S(2)}, u32[]{:S(2)}) collective-permute-start(f32[2,32,128]{2,1,0:T(8,128)S(1)} %get-tuple-element.53), channel_id=1, source_target_pairs={{0,3},{1,0},{2,1},{3,2},{4,7},{5,4},{6,5},{7,6},{8,11},{9,8},{10,9... | collective-permute-start | bytes 98312 | tf_op jit(solution)/shard_map/ppermute | solution.py:29
  279.8 4.8 %collective-permute-start.15 = (f32[2,32,128]{2,1,0:T(8,128)S(1)}, f32[2,32,128]{2,1,0:T(8,128)S(1)}, u32[]{:S(2)}, u32[]{:S(2)}) collective-permute-start(f32[2,32,128]{2,1,0:T(8,128)S(1)} %get-tuple-element.54), channel_id=1, source_target_pairs={{0,2},{1,3},{2,0},{3,1},{4,6},{5,7},{6,4},{7,5},{8,10},{9,11},{10,... | collective-permute-start | bytes 98312 | tf_op jit(solution)/shard_map/ppermute | solution.py:29
